TPU v7x, 128 devices: a whole 4x4x4 slice. The times are simulated.
128 devices in a mesh: sec: 4 (over z), blk: 32 (over x, y, core).
Axes of the slice: x: 4, y: 4, z: 4, core: 2. Of those that a mesh axis runs over, the one named last changes fastest.
Arguments:
- fluid_state: float32 [5, 128, 512, 256], P(None, 'sec', 'blk'), may hold values from -6 to 6
- diffusivity: float32 [128, 512, 256], P('sec', 'blk'), may hold values from 0.2 to 3
- first_jacobian: float32 [5, 5], replicated, may hold values from -1.2 to 1.2
- second_jacobian: float32 [5, 5], replicated, may hold values from -1.2 to 1.2
- wall_normal: float32 [3, 128, 512], P(None, 'sec', 'blk'), may hold values from -6 to 6
- interpolation: float32 [1024, 16, 64, 64], P(('sec', 'blk')), may hold values from -0.75 to 0.75
- target_device: int32 [1024, 16], P(('sec', 'blk')), may hold values from 0 to 127, all different within a row; in each aligned block of 8 rows (0 to 7, 8 to 15, ...) at most 2 rows name the same one
- target_tile: int32 [1024, 16], P(('sec', 'blk')), may hold values from 0 to 15
- live_tiles: int32 [128], P(('sec', 'blk')), may hold values from 1 to 8, as said below
- displacement: float32 [3, 131072], P(None, ('sec', 'blk')), may hold values from -3 to 3
- stiff_diagonal: float32 [3, 131072], P(None, ('sec', 'blk')), may hold values from 1 to 1.5
- stiff_tiles: float32 [2048, 8, 64, 64], P(('sec', 'blk')), may hold values from -0.25 to 0.25
- stiff_columns: int32 [2048, 8], P(('sec', 'blk')), may hold values from 0 to 17
Outputs:
- fluid_field: float32 [5, 128, 512, 256], P(None, 'sec', 'blk')
- final_displacement: float32 [3, 131072], P(None, ('sec', 'blk'))
Inputs may be any that keep to these rules, and one draw needn't show every extreme that they name: `target_device`: each row names 16 different devices; within each device's aligned block of 8 rows no device is named more than 2 times. `live_tiles`: the live tiles of a device are its first that many interface tiles. `stiff_columns`: 0 is the last tile of the device before, 1 to 16 the device's own tiles, 17 the first tile of the device after.
All inputs are finite; a program needn't handle non-finite values.
Results may differ from a plain program's by a relative error of at most 0.0001.
Values sent between devices are 32-bit elements; how exact they have to be, the bound alone decides.
No kernel may reach another device: no remote copies, remote signals or barrier semaphores. Data moves between devices by JAX's collectives and lax.ppermute only.
A program may use at most 192 MiB of HBM per device.

v0:
```python
import jax
import jax.numpy as jnp
from jax import lax
from jax.sharding import PartitionSpec as P

ITERS = 3
SWEEPS = 3


TIME_STEP = 0.04
RELAXATION = 0.5
HIGHEST = lax.Precision.HIGHEST


def with_halo(array, sides, width):
    for axis, dim in sides:
        size, length = (lax.axis_size(axis), array.shape[dim])
        up = [(i, (i + 1) % size) for i in range(size - 1)]
        down = [(j, i) for i, j in up]
        last = lax.slice_in_dim(array, length - width, length, axis=dim)
        first = lax.slice_in_dim(array, 0, width, axis=dim)
        before = lax.ppermute(last, axis, up)
        after = lax.ppermute(first, axis, down)
        array = jnp.concatenate([before, array, after], axis=dim)
    return array


def homogeneous(padded, diffusivity, first_jacobian, second_jacobian):
    centre = padded[:, 1:-1, 1:-1]
    east_side = padded[:, 2:, 1:-1]
    west_side = padded[:, :-2, 1:-1]
    north_side = padded[:, 1:-1, 2:]
    south_side = padded[:, 1:-1, :-2]
    zero_layer = jnp.zeros(centre.shape[:-1] + (1,), jnp.float32)
    upper_side = jnp.concatenate([centre[..., 1:], zero_layer], axis=3)
    lower_side = jnp.concatenate([zero_layer, centre[..., :-1]], axis=3)
    laplace = (
        east_side + west_side + north_side + south_side + upper_side + lower_side - 6.0 * centre
    )
    first_flux = jnp.einsum(
        "cd,dxyz->cxyz", first_jacobian, 0.5 * (east_side - west_side), precision=HIGHEST
    )
    second_flux = jnp.einsum(
        "cd,dxyz->cxyz", second_jacobian, 0.5 * (north_side - south_side), precision=HIGHEST
    )
    return diffusivity[None] * laplace - first_flux - second_flux


def wall_source(motion_plane, diffusivity):
    bottom = motion_plane * diffusivity[None, :, :, 0]
    empty_plane = jnp.zeros_like(bottom[:1])
    ghost_plane = jnp.concatenate([empty_plane, bottom, empty_plane], axis=0)
    depth_index = lax.broadcasted_iota(jnp.int32, (1,) + diffusivity.shape, 3)
    return jnp.where(depth_index == 0, ghost_plane[..., None], 0.0)


def face_rim(field):
    return with_halo(field, (("sec", 1), ("blk", 2)), 1)


def local(
    fluid_state,
    diffusivity,
    first_jacobian,
    second_jacobian,
    wall_normal,
    interpolation,
    target_device,
    target_tile,
    live_tiles,
    displacement,
    stiff_diagonal,
    stiff_tiles,
    stiff_columns,
):
    devices = lax.axis_size(("sec", "blk"))
    wall_tiles = interpolation.shape[0]
    fan_tiles = interpolation.shape[1]
    tile_size = interpolation.shape[2]
    slots_each = 2 * wall_tiles * fan_tiles // devices
    total_slots = devices * slots_each
    pair_count = wall_tiles * fan_tiles
    shell_tiles = displacement.shape[1] // tile_size
    rows_first = fluid_state.shape[1]
    rows_second = fluid_state.shape[2]
    destination = target_device.reshape(pair_count)
    position = jnp.arange(pair_count, dtype=jnp.int32)
    earlier = (destination[:, None] == destination[None, :]) & (
        position[None, :] < position[:, None]
    )
    rank_within = jnp.sum(earlier.astype(jnp.int32), axis=1)
    slot_index = destination * slots_each + rank_within
    slot_match = slot_index[:, None] == jnp.arange(total_slots, dtype=jnp.int32)[None, :]
    slot_table = slot_match.astype(jnp.float32)
    tile_plus = target_tile.reshape(pair_count) + 1
    sent_tiles = jnp.sum(jnp.where(slot_match, tile_plus[:, None], 0), axis=0) - 1
    owned_tiles = lax.all_to_all(
        sent_tiles.reshape(devices, slots_each),
        ("sec", "blk"),
        split_axis=0,
        concat_axis=0,
        tiled=True,
    ).reshape(total_slots)
    owner_table = (
        owned_tiles[:, None] == jnp.arange(shell_tiles, dtype=jnp.int32)[None, :]
    ).astype(jnp.float32)
    live_mask = (jnp.arange(wall_tiles, dtype=jnp.int32) < live_tiles[0]).astype(jnp.float32)
    column_table = (
        stiff_columns[:, :, None] == jnp.arange(shell_tiles + 2, dtype=jnp.int32)[None, None, :]
    ).astype(jnp.float32)

    def send_forth(buffer):
        arrived = lax.all_to_all(buffer, ("sec", "blk"), split_axis=0, concat_axis=0, tiled=True)
        return arrived

    def shell_forces(fluid_field):
        traction = wall_normal * fluid_field[4, :, :, 0][None]
        traction_tiles = traction.reshape(3, wall_tiles, tile_size)
        contribution = jnp.einsum(
            "rkqn,crq->rkcn", interpolation, traction_tiles, precision=HIGHEST
        )
        contribution = contribution * live_mask[:, None, None, None]
        outgoing = jnp.einsum(
            "pm,pcn->mcn",
            slot_table,
            contribution.reshape(pair_count, 3, tile_size),
            precision=HIGHEST,
        )
        arrived = send_forth(outgoing.reshape(devices, slots_each, 3, tile_size)).reshape(
            total_slots, 3, tile_size
        )
        forces = jnp.einsum("ms,mcn->csn", owner_table, arrived, precision=HIGHEST)
        return forces.reshape(3, shell_tiles * tile_size)

    def off_diagonal(values):
        window = with_halo(values, ((("sec", "blk"), 1),), tile_size)
        window_tiles = window.reshape(3, shell_tiles + 2, tile_size)
        chosen = jnp.einsum("ibj,cjn->ibcn", column_table, window_tiles, precision=HIGHEST)
        result = jnp.einsum("ibmn,ibcn->cim", stiff_tiles, chosen, precision=HIGHEST)
        return result.reshape(3, shell_tiles * tile_size)

    def shell_update(current, fluid_field):
        forces = shell_forces(fluid_field)
        estimate = current
        for sweep_index in range(SWEEPS):
            estimate = (forces - off_diagonal(estimate)) / stiff_diagonal
        return (1.0 - RELAXATION) * current + RELAXATION * estimate

    current = displacement
    fluid_field = fluid_state
    base_rate = homogeneous(face_rim(fluid_state), diffusivity, first_jacobian, second_jacobian)
    for iteration in range(ITERS):
        shell_blocks = current.reshape(3, shell_tiles, tile_size)
        reply_tiles = jnp.einsum("ms,csn->mcn", owner_table, shell_blocks, precision=HIGHEST)
        returned = lax.all_to_all(
            reply_tiles.reshape(devices, slots_each, 3, tile_size),
            ("sec", "blk"),
            split_axis=0,
            concat_axis=0,
            tiled=True,
        )
        interface_returned = returned.reshape(total_slots, 3, tile_size)
        pair_values = jnp.einsum("pm,mcn->pcn", slot_table, interface_returned, precision=HIGHEST)
        pair_values = pair_values.reshape(wall_tiles, fan_tiles, 3, tile_size)
        motion = (
            jnp.einsum("rkqn,rkcn->rcq", interpolation, pair_values, precision=HIGHEST)
            * live_mask[:, None, None]
        )
        motion_plane = motion.transpose(1, 0, 2).reshape(3, rows_first, rows_second)
        source = wall_source(motion_plane, diffusivity)
        first_section = fluid_state + TIME_STEP * (base_rate + source)
        later_rate = homogeneous(
            face_rim(first_section), diffusivity, first_jacobian, second_jacobian
        )
        fluid_field = 0.5 * (fluid_state + first_section + TIME_STEP * (later_rate + source))
        current = shell_update(current, fluid_field)
    return (fluid_field, current)


def solution(mesh):
    return jax.shard_map(
        local,
        mesh=mesh,
        in_specs=(
            P(None, "sec", "blk", None),
            P("sec", "blk", None),
            P(),
            P(),
            P(None, "sec", "blk"),
            P(("sec", "blk"), None, None, None),
            P(("sec", "blk"), None),
            P(("sec", "blk"), None),
            P(("sec", "blk")),
            P(None, ("sec", "blk")),
            P(None, ("sec", "blk")),
            P(("sec", "blk"), None, None, None),
            P(("sec", "blk"), None),
        ),
        out_specs=(P(None, "sec", "blk", None), P(None, ("sec", "blk"))),
        check_vma=False,
    )
```

profile of v0, /device:TPU:32, one launch (start us, length us, event | category | flops | bytes accessed | tf_op | source)
XLA Modules:
  0.0 526.0 jit_solution(3766808305172108724)
XLA Ops:
  3.3 10.2 %all-to-all-start = ((s32[128,1,2]{2,1,0:T(1,128)}), s32[128,1,2]{2,1,0:T(1,128)S(1)}, u32[]{:S(2)}, u32[]{:S(2)}) async-start(s32[128,1,2]{2,1,0:T(1,128)} %bitcast.9), calls=%async_computation | async-start | bytes 131072 | tf_op jit(solution)/shard_map/all_to_all | solution.py:97
  28.1 7.9 %collective-permute-start.9 = (f32[3,64]{1,0:T(4,128)S(1)}, f32[3,64]{1,0:T(4,128)S(1)}, u32[]{:S(2)}, u32[]{:S(2)}) collective-permute-start(f32[3,64]{1,0:T(4,128)S(1)} %get-tuple-element.58), channel_id=1, source_target_pairs={{1,0},{2,1},{3,2},{4,3},{5,4},{6,5},{7,6},{8,7},{9,8},{10,9},{11,1... | collective-permute-start | bytes 2312 | tf_op jit(solution)/shard_map/ppermute | solution.py:23
  36.1 8.3 %fusion.185 = (f32[5,32,16,255]{3,0,2,1:T(8,128)}, f32[5,32,16,255]{3,0,2,1:T(8,128)}) fusion(f32[5,32,16,256]{3,0,2,1:T(8,128)} %copy-done.1), kind=kLoop, calls=%fused_computation.273 | loop fusion | bytes 10444800 | tf_op jit(solution)/shard_map/slice | solution.py:35
  52.4 5.5 %all-to-all-start.1 = ((f32[128,1,384]{2,1,0:T(1,128)}), f32[128,1,384]{2,1,0:T(1,128)S(1)}, u32[]{:S(2)}, u32[]{:S(2)}) async-start(f32[128,1,384]{2,1,0:T(1,128)} %reshape.401), calls=%async_computation.1 | async-start | bytes 393216 | tf_op jit(solution)/shard_map/all_to_all | solution.py:155
  69.2 5.7 %fusion.26 = f32[32,16,256,5]{2,3,1,0:T(8,128)} fusion(f32[5,1,16,256]{3,0,2,1:T(8,128)S(1)} %collective-permute-done, f32[5,32,16,256]{3,0,2,1:T(8,128)S(1)} %copy-done.2, f32[5,1,16,256]{3,0,2,1:T(8,128)S(1)} %collective-permute-done.1, f32[5,5]{1,0:T(8,128)S(1)} %copy-done.33), kind=kOutput, calls=%fused_computation.64 | convolution fusion | flops 41943040 | bytes 5406820 | tf_op jit(solution)/shard_map/cd,dxyz->cxyz/dot_general | solution.py:40
  79.5 5.6 %fusion.58 = f32[3,8,64]{2,0,1:T(4,128)S(1)} fusion(f32[8,16,64,64]{3,2,1,0:T(8,128)} %param.18, f32[8,16,3,64]{3,1,2,0:T(8,128)S(1)} %fusion.82, f32[8]{0:T(128)} %compare_convert_fusion), kind=kOutput, calls=%fused_computation.105 | convolution fusion | flops 18875904 | bytes 2201632 | tf_op jit(solution)/shard_map/rkqn,rkcn->rcq/dot_general | solution.py:166
  86.3 23.8 %multiply_add_fusion.1 = (f32[5,32,16,256]{3,0,2,1:T(8,128)S(1)}, f32[5,32,16,256]{3,0,2,1:T(8,128)}, f32[5,32,16,256]{3,0,2,1:T(8,128)}) fusion(f32[5,32,16,256]{3,2,1,0:T(8,128)S(1)} %copy-done.4, f32[5,32,16]{0,2,1:T(8,128)} %copy.272, pred[256]{0:T(512)(128)(4,1)S(1)} %copy-done.50, f32[5,5]{1,0:T(8,128)S(1)} %copy-done, ...), kind=kOutput, calls=%fused_computation.60 | convolution fusion | flops 53739520 | bytes 24783204 | tf_op jit(solution)/shard_map/cd,dxyz->cxyz/dot_general | solution.py:43
  124.7 5.7 %fusion.31 = f32[5,32,16,256]{3,0,2,1:T(8,128)} fusion(f32[5,1,16,256]{3,0,2,1:T(8,128)S(1)} %collective-permute-done.4, f32[5,32,16,256]{3,0,2,1:T(8,128)S(1)} %get-tuple-element.40, f32[5,1,16,256]{3,0,2,1:T(8,128)S(1)} %collective-permute-done.5, f32[5,5]{1,0:T(8,128)S(1)} %copy-done.33), kind=kOutput, calls=%fused_computation.68 | convolution fusion | flops 41943040 | bytes 5406820 | tf_op jit(solution)/shard_map/cd,dxyz->cxyz/dot_general | solution.py:40
  130.4 5.7 %fusion.34 = f32[5,32,16,256]{3,0,2,1:T(8,128)} fusion(f32[5,34,1,256]{3,0,2,1:T(8,128)S(1)} %collective-permute-done.6, f32[5,1,16,256]{3,0,2,1:T(8,128)S(1)} %collective-permute-done.4, f32[5,32,16,256]{3,0,2,1:T(8,128)S(1)} %get-tuple-element.40, f32[5,1,16,256]{3,0,2,1:T(8,128)S(1)} %collective-permute-done.5, ...), kind=kOutput, calls=%fused_computation.69 | convolution fusion | flops 44564480 | bytes 5754980 | tf_op jit(solution)/shard_map/cd,dxyz->cxyz/dot_general | solution.py:43
  136.1 7.5 %subtract_multiply_fusion.1 = f32[5,32,16,256]{3,0,2,1:T(8,128)} fusion(f32[5,32,16,256]{3,0,2,1:T(8,128)S(1)} %get-tuple-element.40, f32[5,32,16,255]{3,0,2,1:T(8,128)} %get-tuple-element.31, f32[5,32,16,255]{3,0,2,1:T(8,128)S(1)} %get-tuple-element.30, f32[5,1,16,256]{3,0,2,1:T(8,128)S(1)} %collective-permute-done.4, ...), kind=kLoop, calls=%fused_computation.59 | loop fusion | flops 10485760 | bytes 11501568 | tf_op jit(solution)/shard_map/mul | solution.py:46
  143.6 5.5 %fusion.75 = f32[1,32,16,1]{3,0,2,1:T(1,128)S(1)} fusion(f32[5,32,16,256]{3,0,2,1:T(8,128)} %get-tuple-element.41, f32[5,32,16,256]{3,0,2,1:T(8,128)} %fusion.34, f32[5,32,16,256]{3,0,2,1:T(8,128)} %fusion.31, f32[5,32,16,256]{3,0,2,1:T(8,128)} %subtract_multiply_fusion.1, f32[5,32,16,256]{3,0,2,1:T(8,128)S(1)} %get-tuple-element.40, ...), kind=kLoop, calls=%fused_computation.139 | loop fusion | flops 3584 | bytes 14336 | tf_op jit(solution)/shard_map/mul | solution.py:175
  149.5 4.3 convolution_multiply_fusion.2
  157.2 14.6 %all-to-all-start.2 = ((f32[128,1,384]{2,1,0:T(1,128)}), f32[128,1,384]{2,1,0:T(1,128)S(1)}, u32[]{:S(2)}, u32[]{:S(2)}) async-start(f32[128,1,384]{2,1,0:T(1,128)} %reshape.403), calls=%async_computation.2 | async-start | bytes 393216 | tf_op jit(solution)/shard_map/all_to_all | solution.py:113
  171.8 6.3 %convolution_bitcast_fusion.8 = f32[16,3,64]{2,1,0:T(4,128)} fusion(f32[16,8,64,64]{3,2,1,0:T(8,128)} %param.24, f32[16,8,3,64]{3,1,2,0:T(8,128)} %fusion.123), kind=kOutput, calls=%fused_computation.93 | convolution fusion | flops 18874368 | bytes 2207744 | tf_op jit(solution)/shard_map/ibmn,ibcn->cim/dot_general | solution.py:139
  188.4 7.9 %collective-permute-start.11 = (f32[3,64]{1,0:T(4,128)S(1)}, f32[3,64]{1,0:T(4,128)S(1)}, u32[]{:S(2)}, u32[]{:S(2)}) collective-permute-start(f32[3,64]{1,0:T(4,128)S(1)} %get-tuple-element.56), channel_id=1, source_target_pairs={{1,0},{2,1},{3,2},{4,3},{5,4},{6,5},{7,6},{8,7},{9,8},{10,9},{11,1... | collective-permute-start | bytes 2312 | tf_op jit(solution)/shard_map/ppermute | solution.py:23
  198.0 5.1 convolution_bitcast_fusion.7
  205.3 7.9 %collective-permute-start.13 = (f32[3,64]{1,0:T(4,128)S(1)}, f32[3,64]{1,0:T(4,128)S(1)}, u32[]{:S(2)}, u32[]{:S(2)}) collective-permute-start(f32[3,64]{1,0:T(4,128)S(1)} %get-tuple-element.54), channel_id=1, source_target_pairs={{1,0},{2,1},{3,2},{4,3},{5,4},{6,5},{7,6},{8,7},{9,8},{10,9},{11,1... | collective-permute-start | bytes 2312 | tf_op jit(solution)/shard_map/ppermute | solution.py:23
  214.9 5.1 convolution_bitcast_fusion.6
  223.4 7.9 %collective-permute-start.19 = (f32[3,64]{1,0:T(4,128)}, f32[3,64]{1,0:T(4,128)}, u32[]{:S(2)}, u32[]{:S(2)}) collective-permute-start(f32[3,64]{1,0:T(4,128)} %get-tuple-element.52), channel_id=1, source_target_pairs={{1,0},{2,1},{3,2},{4,3},{5,4},{6,5},{7,6},{8,7},{9,8},{10,9},{11,1... | collective-permute-start | bytes 2312 | tf_op jit(solution)/shard_map/ppermute | solution.py:23
  240.5 7.8 %all-to-all-done.3 = f32[128,1,384]{2,1,0:T(1,128)S(1)} async-done(((f32[128,1,384]{2,1,0:T(1,128)}), f32[128,1,384]{2,1,0:T(1,128)S(1)}, u32[]{:S(2)}, u32[]{:S(2)}) %all-to-all-start.3) | async-done | bytes 196640 | tf_op jit(solution)/shard_map/all_to_all | solution.py:155
  252.5 5.6 %fusion.56 = f32[3,8,64]{2,0,1:T(4,128)S(1)} fusion(f32[8,16,64,64]{3,2,1,0:T(8,128)} %param.18, f32[8,16,3,64]{3,1,2,0:T(8,128)S(1)} %fusion.80, f32[8]{0:T(128)} %compare_convert_fusion), kind=kOutput, calls=%fused_computation.102 | convolution fusion | flops 18875904 | bytes 2201632 | tf_op jit(solution)/shard_map/rkqn,rkcn->rcq/dot_general | solution.py:166
  258.5 5.8 %multiply_add_fusion = (f32[5,32,16,256]{3,0,2,1:T(8,128)S(1)}, f32[5,32,16,256]{3,0,2,1:T(8,128)}) fusion(f32[5,32,16,256]{3,0,2,1:T(8,128)} %get-tuple-element.60, f32[5,32,16,256]{3,2,1,0:T(8,128)S(1)} %copy-done.4, f32[5,32,16]{0,2,1:T(8,128)S(1)} %copy.294, pred[256]{0:T(512)(128)(4,1)S(1)} %copy-done.51), kind=kLoop, calls=%fused_computation.52 | loop fusion | flops 2621440 | bytes 10496256 | tf_op jit(solution)/shard_map/add | solution.py:171
  279.0 5.7 %fusion.37 = f32[5,32,16,256]{3,0,2,1:T(8,128)} fusion(f32[5,1,16,256]{3,0,2,1:T(8,128)S(1)} %collective-permute-done.14, f32[5,32,16,256]{3,0,2,1:T(8,128)S(1)} %get-tuple-element.38, f32[5,1,16,256]{3,0,2,1:T(8,128)S(1)} %collective-permute-done.15, f32[5,5]{1,0:T(8,128)S(1)} %copy-done.33), kind=kOutput, calls=%fused_computation.70 | convolution fusion | flops 41943040 | bytes 5406820 | tf_op jit(solution)/shard_map/cd,dxyz->cxyz/dot_general | solution.py:40
  284.7 5.7 %fusion.40 = f32[5,32,16,256]{3,0,2,1:T(8,128)} fusion(f32[5,34,1,256]{3,0,2,1:T(8,128)S(1)} %collective-permute-done.16, f32[5,1,16,256]{3,0,2,1:T(8,128)S(1)} %collective-permute-done.14, f32[5,32,16,256]{3,0,2,1:T(8,128)S(1)} %get-tuple-element.38, f32[5,1,16,256]{3,0,2,1:T(8,128)S(1)} %collective-permute-done.15, ...), kind=kOutput, calls=%fused_computation.71 | convolution fusion | flops 44564480 | bytes 5754980 | tf_op jit(solution)/shard_map/cd,dxyz->cxyz/dot_general | solution.py:43
  290.4 7.7 %subtract_multiply_fusion = f32[5,32,16,256]{3,0,2,1:T(8,128)} fusion(f32[5,32,16,256]{3,0,2,1:T(8,128)S(1)} %get-tuple-element.38, f32[5,32,16,255]{3,0,2,1:T(8,128)S(1)} %get-tuple-element.27, f32[5,32,16,255]{3,0,2,1:T(8,128)S(1)} %get-tuple-element.26, f32[5,1,16,256]{3,0,2,1:T(8,128)S(1)} %collective-permute-done.14, ...), kind=kLoop, calls=%fused_computation.51 | loop fusion | flops 10485760 | bytes 11501568 | tf_op jit(solution)/shard_map/mul | solution.py:46
  298.1 5.6 %fusion.76 = f32[1,32,16,1]{3,0,2,1:T(1,128)S(1)} fusion(f32[5,32,16,256]{3,0,2,1:T(8,128)} %get-tuple-element.39, f32[5,32,16,256]{3,0,2,1:T(8,128)} %fusion.40, f32[5,32,16,256]{3,0,2,1:T(8,128)} %fusion.37, f32[5,32,16,256]{3,0,2,1:T(8,128)} %subtract_multiply_fusion, f32[5,32,16,256]{3,0,2,1:T(8,128)S(1)} %get-tuple-element.38, ...), kind=kLoop, calls=%fused_computation.140 | loop fusion | flops 3584 | bytes 14336 | tf_op jit(solution)/shard_map/mul | solution.py:175
  304.1 4.3 convolution_multiply_fusion.1
  311.8 7.6 %all-to-all-start.4 = ((f32[128,1,384]{2,1,0:T(1,128)}), f32[128,1,384]{2,1,0:T(1,128)S(1)}, u32[]{:S(2)}, u32[]{:S(2)}) async-start(f32[128,1,384]{2,1,0:T(1,128)} %reshape.407), calls=%async_computation.4 | async-start | bytes 393216 | tf_op jit(solution)/shard_map/all_to_all | solution.py:113
  319.4 6.3 %convolution_bitcast_fusion.5 = f32[16,3,64]{2,1,0:T(4,128)} fusion(f32[16,8,64,64]{3,2,1,0:T(8,128)} %param.24, f32[16,8,3,64]{3,1,2,0:T(8,128)} %fusion.117), kind=kOutput, calls=%fused_computation.90 | convolution fusion | flops 18874368 | bytes 2207744 | tf_op jit(solution)/shard_map/ibmn,ibcn->cim/dot_general | solution.py:139
  336.0 7.9 %collective-permute-start.21 = (f32[3,64]{1,0:T(4,128)S(1)}, f32[3,64]{1,0:T(4,128)S(1)}, u32[]{:S(2)}, u32[]{:S(2)}) collective-permute-start(f32[3,64]{1,0:T(4,128)S(1)} %get-tuple-element.50), channel_id=1, source_target_pairs={{1,0},{2,1},{3,2},{4,3},{5,4},{6,5},{7,6},{8,7},{9,8},{10,9},{11,1... | collective-permute-start | bytes 2312 | tf_op jit(solution)/shard_map/ppermute | solution.py:23
  345.6 5.1 convolution_bitcast_fusion.4
  352.9 7.9 %collective-permute-start.23 = (f32[3,64]{1,0:T(4,128)S(1)}, f32[3,64]{1,0:T(4,128)S(1)}, u32[]{:S(2)}, u32[]{:S(2)}) collective-permute-start(f32[3,64]{1,0:T(4,128)S(1)} %get-tuple-element.48), channel_id=1, source_target_pairs={{1,0},{2,1},{3,2},{4,3},{5,4},{6,5},{7,6},{8,7},{9,8},{10,9},{11,1... | collective-permute-start | bytes 2312 | tf_op jit(solution)/shard_map/ppermute | solution.py:23
  362.5 5.1 convolution_bitcast_fusion.3
  370.5 7.9 %collective-permute-start.29 = (f32[3,64]{1,0:T(4,128)}, f32[3,64]{1,0:T(4,128)}, u32[]{:S(2)}, u32[]{:S(2)}) collective-permute-start(f32[3,64]{1,0:T(4,128)} %get-tuple-element.46), channel_id=1, source_target_pairs={{1,0},{2,1},{3,2},{4,3},{5,4},{6,5},{7,6},{8,7},{9,8},{10,9},{11,1... | collective-permute-start | bytes 2312 | tf_op jit(solution)/shard_map/ppermute | solution.py:23
  387.5 7.8 %all-to-all-done.5 = f32[128,1,384]{2,1,0:T(1,128)S(1)} async-done(((f32[128,1,384]{2,1,0:T(1,128)}), f32[128,1,384]{2,1,0:T(1,128)S(1)}, u32[]{:S(2)}, u32[]{:S(2)}) %all-to-all-start.5) | async-done | bytes 196640 | tf_op jit(solution)/shard_map/all_to_all | solution.py:155
  399.4 5.6 %fusion.54 = f32[3,8,64]{2,0,1:T(4,128)S(1)} fusion(f32[8,16,64,64]{3,2,1,0:T(8,128)} %param.18, f32[8,16,3,64]{3,1,2,0:T(8,128)S(1)} %fusion.78, f32[8]{0:T(128)} %compare_convert_fusion), kind=kOutput, calls=%fused_computation.99 | convolution fusion | flops 18875904 | bytes 2201632 | tf_op jit(solution)/shard_map/rkqn,rkcn->rcq/dot_general | solution.py:166
  405.5 4.4 fusion.1
  415.8 4.8 fusion.179
  425.2 5.7 %fusion.8 = f32[32,16,256,5]{2,3,1,0:T(8,128)} fusion(f32[5,1,16,256]{3,0,2,1:T(8,128)S(1)} %collective-permute-done.24, f32[5,32,16,256]{3,0,2,1:T(8,128)S(1)} %fusion.1, f32[5,1,16,256]{3,0,2,1:T(8,128)S(1)} %collective-permute-done.25, f32[5,5]{1,0:T(8,128)S(1)} %copy-done.33), kind=kOutput, calls=%fused_computation.42 | convolution fusion | flops 41943040 | bytes 5406820 | tf_op jit(solution)/shard_map/cd,dxyz->cxyz/dot_general | solution.py:40
  431.7 28.9 %fusion.4 = f32[5,32,16,256]{3,0,2,1:T(8,128)} fusion(f32[32,16,256,5]{2,3,1,0:T(8,128)} %fusion.8, f32[5,32,16,256]{3,0,2,1:T(8,128)} %copy-done.3, f32[5,32,16,255]{3,0,2,1:T(8,128)} %get-tuple-element.23, f32[5,32,16,255]{3,0,2,1:T(8,128)} %get-tuple-element.22, f32[5,1,16,256]{3,0,2,1:T(8,128)S(1)} %collective-permute-done.24, ...), kind=kOutput, calls=%fused_computation.6 | convolution fusion | flops 60293120 | bytes 16755044 | tf_op jit(solution)/shard_map/cd,dxyz->cxyz/dot_general | solution.py:43
  469.8 6.8 %all-to-all-start.6 = ((f32[128,1,384]{2,1,0:T(1,128)}), f32[128,1,384]{2,1,0:T(1,128)S(1)}, u32[]{:S(2)}, u32[]{:S(2)}) async-start(f32[128,1,384]{2,1,0:T(1,128)} %reshape.411), calls=%async_computation.6 | async-start | bytes 393216 | tf_op jit(solution)/shard_map/all_to_all | solution.py:113
  476.6 5.1 convolution_bitcast_fusion.2
  481.7 4.6 all-to-all-done.6
  490.2 7.9 %collective-permute-start.31 = (f32[3,64]{1,0:T(4,128)S(1)}, f32[3,64]{1,0:T(4,128)S(1)}, u32[]{:S(2)}, u32[]{:S(2)}) collective-permute-start(f32[3,64]{1,0:T(4,128)S(1)} %get-tuple-element.44), channel_id=1, source_target_pairs={{1,0},{2,1},{3,2},{4,3},{5,4},{6,5},{7,6},{8,7},{9,8},{10,9},{11,1... | collective-permute-start | bytes 2312 | tf_op jit(solution)/shard_map/ppermute | solution.py:23
  499.8 5.1 convolution_bitcast_fusion.1
  507.0 7.9 %collective-permute-start.33 = (f32[3,64]{1,0:T(4,128)S(1)}, f32[3,64]{1,0:T(4,128)S(1)}, u32[]{:S(2)}, u32[]{:S(2)}) collective-permute-start(f32[3,64]{1,0:T(4,128)S(1)} %get-tuple-element.42), channel_id=1, source_target_pairs={{1,0},{2,1},{3,2},{4,3},{5,4},{6,5},{7,6},{8,7},{9,8},{10,9},{11,1... | collective-permute-start | bytes 2312 | tf_op jit(solution)/shard_map/ppermute | solution.py:23
  514.9 4.5 copy.331
  519.9 5.1 convolution_bitcast_fusion
  (351 shorter events, 172.1 us)
Async XLA Ops:
  0.6 85.7 %copy-start = (f32[5,5]{1,0:T(8,128)S(1)}, f32[5,5]{1,0:T(8,128)}, u32[]{:S(2)}) copy-start(f32[5,5]{1,0:T(8,128)} %param.16) | copy-start | bytes 304
  0.6 25.4 %copy-start.30 = (f32[3,1024]{1,0:T(4,128)S(1)}, f32[3,1024]{1,0:T(4,128)}, u32[]{:S(2)}) copy-start(f32[3,1024]{1,0:T(4,128)} %param.22) | copy-start | bytes 36868
  1.6 34.4 %copy-start.46 = (s32[128]{0:T(128)}, s32[128]{0:T(128)S(1)}, u32[]{:S(2)}) copy-start(s32[128]{0:T(128)S(1)} %multiply_add_fusion.5) | copy-start | bytes 1540
  3.3 46.3 %all-to-all-start = ((s32[128,1,2]{2,1,0:T(1,128)}), s32[128,1,2]{2,1,0:T(1,128)S(1)}, u32[]{:S(2)}, u32[]{:S(2)}) async-start(s32[128,1,2]{2,1,0:T(1,128)} %bitcast.9), calls=%async_computation | async-start | bytes 131072 | tf_op jit(solution)/shard_map/all_to_all | solution.py:97
  20.2 40.4 %collective-permute-start = (f32[5,1,16,256]{3,0,2,1:T(8,128)}, f32[5,1,16,256]{3,0,2,1:T(8,128)S(1)}, u32[]{:S(2)}, u32[]{:S(2)}) collective-permute-start(f32[5,1,16,256]{3,0,2,1:T(8,128)} %get-tuple-element.37), channel_id=1, source_target_pairs={{32,0},{64,32},{96,64},{33,1},{65,33},{97,65},{34,2},{66,34},{98,6... | collective-permute-start | bytes 245768 | tf_op jit(solution)/shard_map/ppermute | solution.py:23
  23.1 34.9 %collective-permute-start.1 = (f32[5,1,16,256]{3,0,2,1:T(8,128)}, f32[5,1,16,256]{3,0,2,1:T(8,128)S(1)}, u32[]{:S(2)}, u32[]{:S(2)}) collective-permute-start(f32[5,1,16,256]{3,0,2,1:T(8,128)} %get-tuple-element.36), channel_id=1, source_target_pairs={{0,32},{32,64},{64,96},{1,33},{33,65},{65,97},{2,34},{34,66},{66,9... | collective-permute-start | bytes 245768 | tf_op jit(solution)/shard_map/ppermute | solution.py:22
  26.2 22.2 %collective-permute-start.8 = (f32[3,64]{1,0:T(4,128)S(1)}, f32[3,64]{1,0:T(4,128)S(1)}, u32[]{:S(2)}, u32[]{:S(2)}) collective-permute-start(f32[3,64]{1,0:T(4,128)S(1)} %get-tuple-element.59), channel_id=1, source_target_pairs={{0,1},{1,2},{2,3},{3,4},{4,5},{5,6},{6,7},{7,8},{8,9},{9,10},{10,1... | collective-permute-start | bytes 2312 | tf_op jit(solution)/shard_map/ppermute | solution.py:22
  28.1 20.3 %collective-permute-start.9 = (f32[3,64]{1,0:T(4,128)S(1)}, f32[3,64]{1,0:T(4,128)S(1)}, u32[]{:S(2)}, u32[]{:S(2)}) collective-permute-start(f32[3,64]{1,0:T(4,128)S(1)} %get-tuple-element.58), channel_id=1, source_target_pairs={{1,0},{2,1},{3,2},{4,3},{5,4},{6,5},{7,6},{8,7},{9,8},{10,9},{11,1... | collective-permute-start | bytes 2312 | tf_op jit(solution)/shard_map/ppermute | solution.py:23
  52.4 22.4 %all-to-all-start.1 = ((f32[128,1,384]{2,1,0:T(1,128)}), f32[128,1,384]{2,1,0:T(1,128)S(1)}, u32[]{:S(2)}, u32[]{:S(2)}) async-start(f32[128,1,384]{2,1,0:T(1,128)} %reshape.401), calls=%async_computation.1 | async-start | bytes 393216 | tf_op jit(solution)/shard_map/all_to_all | solution.py:155
  63.6 22.7 %collective-permute-start.2 = (f32[5,34,1,256]{3,0,2,1:T(8,128)}, f32[5,34,1,256]{3,0,2,1:T(8,128)}, u32[]{:S(2)}, u32[]{:S(2)}) collective-permute-start(f32[5,34,1,256]{3,0,2,1:T(8,128)} %get-tuple-element.21), channel_id=1, source_target_pairs={{1,0},{2,1},{3,2},{4,3},{5,4},{6,5},{7,6},{8,7},{9,8},{10,9},{11,1... | collective-permute-start | bytes 522248 | tf_op jit(solution)/shard_map/ppermute | solution.py:23
  64.9 21.4 %collective-permute-start.3 = (f32[5,34,1,256]{3,0,2,1:T(8,128)}, f32[5,34,1,256]{3,0,2,1:T(8,128)}, u32[]{:S(2)}, u32[]{:S(2)}) collective-permute-start(f32[5,34,1,256]{3,0,2,1:T(8,128)} %get-tuple-element.20), channel_id=1, source_target_pairs={{0,1},{1,2},{2,3},{3,4},{4,5},{5,6},{6,7},{7,8},{8,9},{9,10},{10,1... | collective-permute-start | bytes 522248 | tf_op jit(solution)/shard_map/ppermute | solution.py:22
  85.3 24.9 %copy-start.25 = (f32[1,32,16]{2,1,0:T(8,128)}, f32[1,32,16]{2,1,0:T(8,128)S(1)}, u32[]{:S(2)}) copy-start(f32[1,32,16]{2,1,0:T(8,128)S(1)} %broadcast.192) | copy-start | bytes 6148
  110.2 9.5 %collective-permute-start.4 = (f32[5,1,16,256]{3,0,2,1:T(8,128)S(1)}, f32[5,1,16,256]{3,0,2,1:T(8,128)S(1)}, u32[]{:S(2)}, u32[]{:S(2)}) collective-permute-start(f32[5,1,16,256]{3,0,2,1:T(8,128)S(1)} %get-tuple-element.33), channel_id=1, source_target_pairs={{32,0},{64,32},{96,64},{33,1},{65,33},{97,65},{34,2},{66,34},{98,6... | collective-permute-start | bytes 245768 | tf_op jit(solution)/shard_map/ppermute | solution.py:23
  113.1 7.0 %collective-permute-start.5 = (f32[5,1,16,256]{3,0,2,1:T(8,128)S(1)}, f32[5,1,16,256]{3,0,2,1:T(8,128)S(1)}, u32[]{:S(2)}, u32[]{:S(2)}) collective-permute-start(f32[5,1,16,256]{3,0,2,1:T(8,128)S(1)} %get-tuple-element.32), channel_id=1, source_target_pairs={{0,32},{32,64},{64,96},{1,33},{33,65},{65,97},{2,34},{34,66},{66,9... | collective-permute-start | bytes 245768 | tf_op jit(solution)/shard_map/ppermute | solution.py:22
  120.2 10.2 %collective-permute-start.6 = (f32[5,34,1,256]{3,0,2,1:T(8,128)S(1)}, f32[5,34,1,256]{3,0,2,1:T(8,128)S(1)}, u32[]{:S(2)}, u32[]{:S(2)}) collective-permute-start(f32[5,34,1,256]{3,0,2,1:T(8,128)S(1)} %get-tuple-element.19), channel_id=1, source_target_pairs={{1,0},{2,1},{3,2},{4,3},{5,4},{6,5},{7,6},{8,7},{9,8},{10,9},{11,1... | collective-permute-start | bytes 522248 | tf_op jit(solution)/shard_map/ppermute | solution.py:23
  121.5 8.9 %collective-permute-start.7 = (f32[5,34,1,256]{3,0,2,1:T(8,128)S(1)}, f32[5,34,1,256]{3,0,2,1:T(8,128)S(1)}, u32[]{:S(2)}, u32[]{:S(2)}) collective-permute-start(f32[5,34,1,256]{3,0,2,1:T(8,128)S(1)} %get-tuple-element.18), channel_id=1, source_target_pairs={{0,1},{1,2},{2,3},{3,4},{4,5},{5,6},{6,7},{7,8},{8,9},{9,10},{10,1... | collective-permute-start | bytes 522248 | tf_op jit(solution)/shard_map/ppermute | solution.py:22
  157.2 24.3 %all-to-all-start.2 = ((f32[128,1,384]{2,1,0:T(1,128)}), f32[128,1,384]{2,1,0:T(1,128)S(1)}, u32[]{:S(2)}, u32[]{:S(2)}) async-start(f32[128,1,384]{2,1,0:T(1,128)} %reshape.403), calls=%async_computation.2 | async-start | bytes 393216 | tf_op jit(solution)/shard_map/all_to_all | solution.py:113
  186.5 9.8 %collective-permute-start.10 = (f32[3,64]{1,0:T(4,128)S(1)}, f32[3,64]{1,0:T(4,128)S(1)}, u32[]{:S(2)}, u32[]{:S(2)}) collective-permute-start(f32[3,64]{1,0:T(4,128)S(1)} %get-tuple-element.57), channel_id=1, source_target_pairs={{0,1},{1,2},{2,3},{3,4},{4,5},{5,6},{6,7},{7,8},{8,9},{9,10},{10,1... | collective-permute-start | bytes 2312 | tf_op jit(solution)/shard_map/ppermute | solution.py:22
  188.4 9.2 %collective-permute-start.11 = (f32[3,64]{1,0:T(4,128)S(1)}, f32[3,64]{1,0:T(4,128)S(1)}, u32[]{:S(2)}, u32[]{:S(2)}) collective-permute-start(f32[3,64]{1,0:T(4,128)S(1)} %get-tuple-element.56), channel_id=1, source_target_pairs={{1,0},{2,1},{3,2},{4,3},{5,4},{6,5},{7,6},{8,7},{9,8},{10,9},{11,1... | collective-permute-start | bytes 2312 | tf_op jit(solution)/shard_map/ppermute | solution.py:23
  198.0 33.2 %copy-start.39 = (s32[128,2]{0,1:T(2,128)S(1)}, s32[128,2]{0,1:T(2,128)}, u32[]{:S(2)}) copy-start(s32[128,2]{0,1:T(2,128)} %copy-done.38) | copy-start | bytes 3076
  203.4 9.8 %collective-permute-start.12 = (f32[3,64]{1,0:T(4,128)S(1)}, f32[3,64]{1,0:T(4,128)S(1)}, u32[]{:S(2)}, u32[]{:S(2)}) collective-permute-start(f32[3,64]{1,0:T(4,128)S(1)} %get-tuple-element.55), channel_id=1, source_target_pairs={{0,1},{1,2},{2,3},{3,4},{4,5},{5,6},{6,7},{7,8},{8,9},{9,10},{10,1... | collective-permute-start | bytes 2312 | tf_op jit(solution)/shard_map/ppermute | solution.py:22
  205.3 9.2 %collective-permute-start.13 = (f32[3,64]{1,0:T(4,128)S(1)}, f32[3,64]{1,0:T(4,128)S(1)}, u32[]{:S(2)}, u32[]{:S(2)}) collective-permute-start(f32[3,64]{1,0:T(4,128)S(1)} %get-tuple-element.54), channel_id=1, source_target_pairs={{1,0},{2,1},{3,2},{4,3},{5,4},{6,5},{7,6},{8,7},{9,8},{10,9},{11,1... | collective-permute-start | bytes 2312 | tf_op jit(solution)/shard_map/ppermute | solution.py:23
  221.5 17.2 %collective-permute-start.18 = (f32[3,64]{1,0:T(4,128)}, f32[3,64]{1,0:T(4,128)}, u32[]{:S(2)}, u32[]{:S(2)}) collective-permute-start(f32[3,64]{1,0:T(4,128)} %get-tuple-element.53), channel_id=1, source_target_pairs={{0,1},{1,2},{2,3},{3,4},{4,5},{5,6},{6,7},{7,8},{8,9},{9,10},{10,1... | collective-permute-start | bytes 2312 | tf_op jit(solution)/shard_map/ppermute | solution.py:22
  223.4 15.3 %collective-permute-start.19 = (f32[3,64]{1,0:T(4,128)}, f32[3,64]{1,0:T(4,128)}, u32[]{:S(2)}, u32[]{:S(2)}) collective-permute-start(f32[3,64]{1,0:T(4,128)} %get-tuple-element.52), channel_id=1, source_target_pairs={{1,0},{2,1},{3,2},{4,3},{5,4},{6,5},{7,6},{8,7},{9,8},{10,9},{11,1... | collective-permute-start | bytes 2312 | tf_op jit(solution)/shard_map/ppermute | solution.py:23
  234.5 13.8 %all-to-all-start.3 = ((f32[128,1,384]{2,1,0:T(1,128)}), f32[128,1,384]{2,1,0:T(1,128)S(1)}, u32[]{:S(2)}, u32[]{:S(2)}) async-start(f32[128,1,384]{2,1,0:T(1,128)} %reshape.405), calls=%async_computation.3 | async-start | bytes 393216 | tf_op jit(solution)/shard_map/all_to_all | solution.py:155
  264.3 7.4 %collective-permute-start.14 = (f32[5,1,16,256]{3,0,2,1:T(8,128)S(1)}, f32[5,1,16,256]{3,0,2,1:T(8,128)S(1)}, u32[]{:S(2)}, u32[]{:S(2)}) collective-permute-start(f32[5,1,16,256]{3,0,2,1:T(8,128)S(1)} %get-tuple-element.29), channel_id=1, source_target_pairs={{32,0},{64,32},{96,64},{33,1},{65,33},{97,65},{34,2},{66,34},{98,6... | collective-permute-start | bytes 245768 | tf_op jit(solution)/shard_map/ppermute | solution.py:23
  267.5 6.9 %collective-permute-start.15 = (f32[5,1,16,256]{3,0,2,1:T(8,128)S(1)}, f32[5,1,16,256]{3,0,2,1:T(8,128)S(1)}, u32[]{:S(2)}, u32[]{:S(2)}) collective-permute-start(f32[5,1,16,256]{3,0,2,1:T(8,128)S(1)} %get-tuple-element.28), channel_id=1, source_target_pairs={{0,32},{32,64},{64,96},{1,33},{33,65},{65,97},{2,34},{34,66},{66,9... | collective-permute-start | bytes 245768 | tf_op jit(solution)/shard_map/ppermute | solution.py:22
  274.4 10.2 %collective-permute-start.16 = (f32[5,34,1,256]{3,0,2,1:T(8,128)S(1)}, f32[5,34,1,256]{3,0,2,1:T(8,128)S(1)}, u32[]{:S(2)}, u32[]{:S(2)}) collective-permute-start(f32[5,34,1,256]{3,0,2,1:T(8,128)S(1)} %get-tuple-element.17), channel_id=1, source_target_pairs={{1,0},{2,1},{3,2},{4,3},{5,4},{6,5},{7,6},{8,7},{9,8},{10,9},{11,1... | collective-permute-start | bytes 522248 | tf_op jit(solution)/shard_map/ppermute | solution.py:23
  275.8 8.9 %collective-permute-start.17 = (f32[5,34,1,256]{3,0,2,1:T(8,128)S(1)}, f32[5,34,1,256]{3,0,2,1:T(8,128)S(1)}, u32[]{:S(2)}, u32[]{:S(2)}) collective-permute-start(f32[5,34,1,256]{3,0,2,1:T(8,128)S(1)} %get-tuple-element.16), channel_id=1, source_target_pairs={{0,1},{1,2},{2,3},{3,4},{4,5},{5,6},{6,7},{7,8},{8,9},{9,10},{10,1... | collective-permute-start | bytes 522248 | tf_op jit(solution)/shard_map/ppermute | solution.py:22
  311.8 17.3 %all-to-all-start.4 = ((f32[128,1,384]{2,1,0:T(1,128)}), f32[128,1,384]{2,1,0:T(1,128)S(1)}, u32[]{:S(2)}, u32[]{:S(2)}) async-start(f32[128,1,384]{2,1,0:T(1,128)} %reshape.407), calls=%async_computation.4 | async-start | bytes 393216 | tf_op jit(solution)/shard_map/all_to_all | solution.py:113
  334.1 9.8 %collective-permute-start.20 = (f32[3,64]{1,0:T(4,128)S(1)}, f32[3,64]{1,0:T(4,128)S(1)}, u32[]{:S(2)}, u32[]{:S(2)}) collective-permute-start(f32[3,64]{1,0:T(4,128)S(1)} %get-tuple-element.51), channel_id=1, source_target_pairs={{0,1},{1,2},{2,3},{3,4},{4,5},{5,6},{6,7},{7,8},{8,9},{9,10},{10,1... | collective-permute-start | bytes 2312 | tf_op jit(solution)/shard_map/ppermute | solution.py:22
  336.0 9.2 %collective-permute-start.21 = (f32[3,64]{1,0:T(4,128)S(1)}, f32[3,64]{1,0:T(4,128)S(1)}, u32[]{:S(2)}, u32[]{:S(2)}) collective-permute-start(f32[3,64]{1,0:T(4,128)S(1)} %get-tuple-element.50), channel_id=1, source_target_pairs={{1,0},{2,1},{3,2},{4,3},{5,4},{6,5},{7,6},{8,7},{9,8},{10,9},{11,1... | collective-permute-start | bytes 2312 | tf_op jit(solution)/shard_map/ppermute | solution.py:23
  345.6 32.7 %copy-start.40 = (s32[128,2]{0,1:T(2,128)S(1)}, s32[128,2]{0,1:T(2,128)}, u32[]{:S(2)}) copy-start(s32[128,2]{0,1:T(2,128)} %copy-done.38) | copy-start | bytes 3076
  351.0 9.8 %collective-permute-start.22 = (f32[3,64]{1,0:T(4,128)S(1)}, f32[3,64]{1,0:T(4,128)S(1)}, u32[]{:S(2)}, u32[]{:S(2)}) collective-permute-start(f32[3,64]{1,0:T(4,128)S(1)} %get-tuple-element.49), channel_id=1, source_target_pairs={{0,1},{1,2},{2,3},{3,4},{4,5},{5,6},{6,7},{7,8},{8,9},{9,10},{10,1... | collective-permute-start | bytes 2312 | tf_op jit(solution)/shard_map/ppermute | solution.py:22
  352.9 9.2 %collective-permute-start.23 = (f32[3,64]{1,0:T(4,128)S(1)}, f32[3,64]{1,0:T(4,128)S(1)}, u32[]{:S(2)}, u32[]{:S(2)}) collective-permute-start(f32[3,64]{1,0:T(4,128)S(1)} %get-tuple-element.48), channel_id=1, source_target_pairs={{1,0},{2,1},{3,2},{4,3},{5,4},{6,5},{7,6},{8,7},{9,8},{10,9},{11,1... | collective-permute-start | bytes 2312 | tf_op jit(solution)/shard_map/ppermute | solution.py:23
  368.5 17.1 %collective-permute-start.28 = (f32[3,64]{1,0:T(4,128)}, f32[3,64]{1,0:T(4,128)}, u32[]{:S(2)}, u32[]{:S(2)}) collective-permute-start(f32[3,64]{1,0:T(4,128)} %get-tuple-element.47), channel_id=1, source_target_pairs={{0,1},{1,2},{2,3},{3,4},{4,5},{5,6},{6,7},{7,8},{8,9},{9,10},{10,1... | collective-permute-start | bytes 2312 | tf_op jit(solution)/shard_map/ppermute | solution.py:22
  370.5 15.2 %collective-permute-start.29 = (f32[3,64]{1,0:T(4,128)}, f32[3,64]{1,0:T(4,128)}, u32[]{:S(2)}, u32[]{:S(2)}) collective-permute-start(f32[3,64]{1,0:T(4,128)} %get-tuple-element.46), channel_id=1, source_target_pairs={{1,0},{2,1},{3,2},{4,3},{5,4},{6,5},{7,6},{8,7},{9,8},{10,9},{11,1... | collective-permute-start | bytes 2312 | tf_op jit(solution)/shard_map/ppermute | solution.py:23
  381.6 13.7 %all-to-all-start.5 = ((f32[128,1,384]{2,1,0:T(1,128)}), f32[128,1,384]{2,1,0:T(1,128)S(1)}, u32[]{:S(2)}, u32[]{:S(2)}) async-start(f32[128,1,384]{2,1,0:T(1,128)} %reshape.409), calls=%async_computation.5 | async-start | bytes 393216 | tf_op jit(solution)/shard_map/all_to_all | solution.py:155
  409.9 10.7 %collective-permute-start.24 = (f32[5,1,16,256]{3,0,2,1:T(8,128)S(1)}, f32[5,1,16,256]{3,0,2,1:T(8,128)S(1)}, u32[]{:S(2)}, u32[]{:S(2)}) collective-permute-start(f32[5,1,16,256]{3,0,2,1:T(8,128)S(1)} %get-tuple-element.25), channel_id=1, source_target_pairs={{32,0},{64,32},{96,64},{33,1},{65,33},{97,65},{34,2},{66,34},{98,6... | collective-permute-start | bytes 245768 | tf_op jit(solution)/shard_map/ppermute | solution.py:23
  413.0 7.6 %collective-permute-start.25 = (f32[5,1,16,256]{3,0,2,1:T(8,128)S(1)}, f32[5,1,16,256]{3,0,2,1:T(8,128)S(1)}, u32[]{:S(2)}, u32[]{:S(2)}) collective-permute-start(f32[5,1,16,256]{3,0,2,1:T(8,128)S(1)} %get-tuple-element.24), channel_id=1, source_target_pairs={{0,32},{32,64},{64,96},{1,33},{33,65},{65,97},{2,34},{34,66},{66,9... | collective-permute-start | bytes 245768 | tf_op jit(solution)/shard_map/ppermute | solution.py:22
  420.6 10.3 %collective-permute-start.26 = (f32[5,34,1,256]{3,0,2,1:T(8,128)S(1)}, f32[5,34,1,256]{3,0,2,1:T(8,128)S(1)}, u32[]{:S(2)}, u32[]{:S(2)}) collective-permute-start(f32[5,34,1,256]{3,0,2,1:T(8,128)S(1)} %get-tuple-element.15), channel_id=1, source_target_pairs={{1,0},{2,1},{3,2},{4,3},{5,4},{6,5},{7,6},{8,7},{9,8},{10,9},{11,1... | collective-permute-start | bytes 522248 | tf_op jit(solution)/shard_map/ppermute | solution.py:23
  421.9 9.0 %collective-permute-start.27 = (f32[5,34,1,256]{3,0,2,1:T(8,128)S(1)}, f32[5,34,1,256]{3,0,2,1:T(8,128)S(1)}, u32[]{:S(2)}, u32[]{:S(2)}) collective-permute-start(f32[5,34,1,256]{3,0,2,1:T(8,128)S(1)} %get-tuple-element.14), channel_id=1, source_target_pairs={{0,1},{1,2},{2,3},{3,4},{4,5},{5,6},{6,7},{7,8},{8,9},{9,10},{10,1... | collective-permute-start | bytes 522248 | tf_op jit(solution)/shard_map/ppermute | solution.py:22
  431.7 32.0 %copy-start.37 = (f32[8]{0:T(128)S(1)}, f32[8]{0:T(128)}, u32[]{:S(2)}) copy-start(f32[8]{0:T(128)} %compare_convert_fusion) | copy-start | bytes 100
  469.8 16.6 %all-to-all-start.6 = ((f32[128,1,384]{2,1,0:T(1,128)}), f32[128,1,384]{2,1,0:T(1,128)S(1)}, u32[]{:S(2)}, u32[]{:S(2)}) async-start(f32[128,1,384]{2,1,0:T(1,128)} %reshape.411), calls=%async_computation.6 | async-start | bytes 393216 | tf_op jit(solution)/shard_map/all_to_all | solution.py:113
  488.2 9.8 %collective-permute-start.30 = (f32[3,64]{1,0:T(4,128)S(1)}, f32[3,64]{1,0:T(4,128)S(1)}, u32[]{:S(2)}, u32[]{:S(2)}) collective-permute-start(f32[3,64]{1,0:T(4,128)S(1)} %get-tuple-element.45), channel_id=1, source_target_pairs={{0,1},{1,2},{2,3},{3,4},{4,5},{5,6},{6,7},{7,8},{8,9},{9,10},{10,1... | collective-permute-start | bytes 2312 | tf_op jit(solution)/shard_map/ppermute | solution.py:22
  490.2 9.2 %collective-permute-start.31 = (f32[3,64]{1,0:T(4,128)S(1)}, f32[3,64]{1,0:T(4,128)S(1)}, u32[]{:S(2)}, u32[]{:S(2)}) collective-permute-start(f32[3,64]{1,0:T(4,128)S(1)} %get-tuple-element.44), channel_id=1, source_target_pairs={{1,0},{2,1},{3,2},{4,3},{5,4},{6,5},{7,6},{8,7},{9,8},{10,9},{11,1... | collective-permute-start | bytes 2312 | tf_op jit(solution)/shard_map/ppermute | solution.py:23
  505.1 14.3 %collective-permute-start.32 = (f32[3,64]{1,0:T(4,128)S(1)}, f32[3,64]{1,0:T(4,128)S(1)}, u32[]{:S(2)}, u32[]{:S(2)}) collective-permute-start(f32[3,64]{1,0:T(4,128)S(1)} %get-tuple-element.43), channel_id=1, source_target_pairs={{0,1},{1,2},{2,3},{3,4},{4,5},{5,6},{6,7},{7,8},{8,9},{9,10},{10,1... | collective-permute-start | bytes 2312 | tf_op jit(solution)/shard_map/ppermute | solution.py:22
  507.0 12.4 %collective-permute-start.33 = (f32[3,64]{1,0:T(4,128)S(1)}, f32[3,64]{1,0:T(4,128)S(1)}, u32[]{:S(2)}, u32[]{:S(2)}) collective-permute-start(f32[3,64]{1,0:T(4,128)S(1)} %get-tuple-element.42), channel_id=1, source_target_pairs={{1,0},{2,1},{3,2},{4,3},{5,4},{6,5},{7,6},{8,7},{9,8},{10,9},{11,1... | collective-permute-start | bytes 2312 | tf_op jit(solution)/shard_map/ppermute | solution.py:23
  (50 other events, 523.7 us)
where the time goes:
time: 536 us; the launch traced here: 526 us
  starting transfers between devices  183 us (34%)
  matrix products  180 us (34%)
  local copies, waits for them, and re-layouts  71.5 us (13%)
  other arithmetic  54.2 us (10%)
  waiting for transfers between devices  34.3 us (6%)
    ppermute x17, starting transfers between devices, with_halo(): after = lax.ppermute(first, axis, down)  87.8 us
    dot_general x4, matrix products, homogeneous(): jnp.einsum('cd,dxyz->cxyz', second_jacobian, 0.5 * (north_side - south_si...  64.1 us
    dot_general x9, matrix products, off_diagonal(): jnp.einsum('ibmn,ibcn->cim', stiff_tiles, chosen, precision=HIGHEST)  48.6 us
    ppermute x17, starting transfers between devices, with_halo(): before = lax.ppermute(last, axis, up)  42.5 us
    unnamed x129, local copies, waits for them, and re-layouts  30.2 us
    all_to_all x3, starting transfers between devices, send_forth(): lax.all_to_all(buffer, ('sec', 'blk'), split_axis=0, concat_axis=0, tiled...  29 us
    dot_general x4, matrix products, homogeneous(): jnp.einsum('cd,dxyz->cxyz', first_jacobian, 0.5 * (east_side - west_side)...  22.8 us
    slice x4, local copies, waits for them, and re-layouts, homogeneous(): upper_side = jnp.concatenate([centre[..., 1:], zero_layer], axis=3)  18.3 us
  transfers between devices with their start and end apart: 41, of which 12 were waited for; matrix products, arithmetic and copies ran while one was open for 19% of the time, Pallas kernels for 0%

commit v1 on v0

--- a/solution.py
+++ b/solution.py
@@ -46,16 +46,22 @@
     return diffusivity[None] * laplace - first_flux - second_flux
 
 
-def wall_source(motion_plane, diffusivity):
-    bottom = motion_plane * diffusivity[None, :, :, 0]
-    empty_plane = jnp.zeros_like(bottom[:1])
-    ghost_plane = jnp.concatenate([empty_plane, bottom, empty_plane], axis=0)
-    depth_index = lax.broadcasted_iota(jnp.int32, (1,) + diffusivity.shape, 3)
-    return jnp.where(depth_index == 0, ghost_plane[..., None], 0.0)
-
-
 def face_rim(field):
     return with_halo(field, (("sec", 1), ("blk", 2)), 1)
+
+
+def plane_sides(plane):
+    sides = []
+    for axis, dim in (("sec", 1), ("blk", 2)):
+        size, length = (lax.axis_size(axis), plane.shape[dim])
+        up = [(i, i + 1) for i in range(size - 1)]
+        down = [(j, i) for i, j in up]
+        before = lax.ppermute(lax.slice_in_dim(plane, length - 1, length, axis=dim), axis, up)
+        after = lax.ppermute(lax.slice_in_dim(plane, 0, 1, axis=dim), axis, down)
+        ahead = jnp.concatenate([lax.slice_in_dim(plane, 1, length, axis=dim), after], axis=dim)
+        behind = jnp.concatenate([before, lax.slice_in_dim(plane, 0, length - 1, axis=dim)], axis=dim)
+        sides.append((ahead, behind))
+    return sides
 
 
 def local(
@@ -113,8 +119,8 @@
         arrived = lax.all_to_all(buffer, ("sec", "blk"), split_axis=0, concat_axis=0, tiled=True)
         return arrived
 
-    def shell_forces(fluid_field):
-        traction = wall_normal * fluid_field[4, :, :, 0][None]
+    def shell_forces(wall_value):
+        traction = wall_normal * wall_value[None]
         traction_tiles = traction.reshape(3, wall_tiles, tile_size)
         contribution = jnp.einsum(
             "rkqn,crq->rkcn", interpolation, traction_tiles, precision=HIGHEST
@@ -139,16 +145,39 @@
         result = jnp.einsum("ibmn,ibcn->cim", stiff_tiles, chosen, precision=HIGHEST)
         return result.reshape(3, shell_tiles * tile_size)
 
-    def shell_update(current, fluid_field):
-        forces = shell_forces(fluid_field)
+    def shell_update(current, wall_value):
+        forces = shell_forces(wall_value)
         estimate = current
         for sweep_index in range(SWEEPS):
             estimate = (forces - off_diagonal(estimate)) / stiff_diagonal
         return (1.0 - RELAXATION) * current + RELAXATION * estimate
 
+    wall_bottom = diffusivity[:, :, 0]
+    wall_above = diffusivity[:, :, 1]
+    first_section = fluid_state + TIME_STEP * homogeneous(
+        face_rim(fluid_state), diffusivity, first_jacobian, second_jacobian
+    )
+    settled = 0.5 * (
+        fluid_state
+        + first_section
+        + TIME_STEP
+        * homogeneous(face_rim(first_section), diffusivity, first_jacobian, second_jacobian)
+    )
+    settled_wall = settled[4, :, :, 0]
+    half_square = 0.5 * TIME_STEP * TIME_STEP
+
+    def wall_state(motion_plane):
+        source = motion_plane * wall_bottom[None]
+        (east_side, west_side), (north_side, south_side) = plane_sides(source)
+        first_flux = jnp.einsum(
+            "cd,dxy->cxy", first_jacobian[:, 1:4], 0.5 * (east_side - west_side), precision=HIGHEST
+        )
+        second_flux = jnp.einsum(
+            "cd,dxy->cxy", second_jacobian[:, 1:4], 0.5 * (north_side - south_side), precision=HIGHEST
+        )
+        return source, east_side + west_side + north_side + south_side, first_flux, second_flux
+
     current = displacement
-    fluid_field = fluid_state
-    base_rate = homogeneous(face_rim(fluid_state), diffusivity, first_jacobian, second_jacobian)
     for iteration in range(ITERS):
         shell_blocks = current.reshape(3, shell_tiles, tile_size)
         reply_tiles = jnp.einsum("ms,csn->mcn", owner_table, shell_blocks, precision=HIGHEST)
@@ -167,13 +196,22 @@
             * live_mask[:, None, None]
         )
         motion_plane = motion.transpose(1, 0, 2).reshape(3, rows_first, rows_second)
-        source = wall_source(motion_plane, diffusivity)
-        first_section = fluid_state + TIME_STEP * (base_rate + source)
-        later_rate = homogeneous(
-            face_rim(first_section), diffusivity, first_jacobian, second_jacobian
-        )
-        fluid_field = 0.5 * (fluid_state + first_section + TIME_STEP * (later_rate + source))
-        current = shell_update(current, fluid_field)
+        source, neighbours, first_flux, second_flux = wall_state(motion_plane)
+        wall_value = settled_wall - half_square * (first_flux[4] + second_flux[4])
+        current = shell_update(current, wall_value)
+    bottom = TIME_STEP * source + half_square * (
+        wall_bottom[None] * (neighbours - 6.0 * source) - first_flux[1:4] - second_flux[1:4]
+    )
+    above = half_square * wall_above[None] * source
+    zero_plane = jnp.zeros_like(source[:1])
+    bottom = jnp.concatenate([zero_plane, bottom, zero_plane], axis=0)
+    bottom = bottom.at[0].add(-half_square * (first_flux[0] + second_flux[0]))
+    bottom = bottom.at[4].add(-half_square * (first_flux[4] + second_flux[4]))
+    above = jnp.concatenate([zero_plane, above, zero_plane], axis=0)
+    edge = jnp.stack([bottom, above], axis=3)
+    fluid_field = lax.dynamic_update_slice(
+        settled, settled[:, :, :, 0:2] + edge, (0, 0, 0, 0)
+    )
     return (fluid_field, current)
 
 

time: 536 us -> 490 us (0.914)
  other arithmetic: 54.2 us -> 11.6 us
  matrix products: 180 us -> 150 us
  starting transfers between devices: 183 us -> 200 us
  local copies, waits for them, and re-layouts: 71.5 us -> 77.9 us
    ppermute x0 -> x12, starting transfers between devices: none -> 30.9 us  [the longest x6 18 us: plane_sides(): lax.ppermute(lax.slice_in_dim(plane, length - 1, length, axis=dim), axis,...]
    mul x10 -> x16, other arithmetic: 27.1 us -> 1.09 us  [the longest x6 0.75 us: shell_forces(): traction = wall_normal * wall_value[None]]
    dynamic_update_slice x0 -> x1, local copies, waits for them, and re-layouts: none -> 14.9 us  [local(): lax.dynamic_update_slice(settled, settled[:, :, :, 0:2] + edge, (0, 0, 0,...]
    dot_general x4 -> x2, matrix products: 64.1 us -> 51.7 us  [homogeneous(): jnp.einsum('cd,dxyz->cxyz', second_jacobian, 0.5 * (north_side - south_si...]
    ppermute x17 -> x13, starting transfers between devices: 42.5 us -> 32.2 us  [with_halo(): before = lax.ppermute(last, axis, up)]
    add x2, other arithmetic: 10.2 us -> 0.12 us  [the longest x1 0.1 us: local(): TIME_STEP * source]
    dot_general x4 -> x2, matrix products: 22.8 us -> 12.8 us  [homogeneous(): jnp.einsum('cd,dxyz->cxyz', first_jacobian, 0.5 * (east_side - west_side)...]
    ppermute x17 -> x13, starting transfers between devices: 87.8 us -> 78.2 us  [with_halo(): after = lax.ppermute(first, axis, down)]
  transfers between devices with their start and end apart: 41 -> 45, of which waited for: 12 -> 12; matrix products, arithmetic and copies ran while one was open for 19% -> 21% of each run, Pallas kernels for 0% -> 0%
where the time goes in v1:
time: 490 us; the launch traced here: 480 us
  starting transfers between devices  200 us (41%)
  matrix products  150 us (31%)
  local copies, waits for them, and re-layouts  77.9 us (16%)
  waiting for transfers between devices  36.9 us (8%)
  other arithmetic  11.6 us (2%)
    ppermute x13, starting transfers between devices, with_halo(): after = lax.ppermute(first, axis, down)  78.2 us
    dot_general x2, matrix products, homogeneous(): jnp.einsum('cd,dxyz->cxyz', second_jacobian, 0.5 * (north_side - south_si...  51.7 us
    dot_general x9, matrix products, off_diagonal(): jnp.einsum('ibmn,ibcn->cim', stiff_tiles, chosen, precision=HIGHEST)  46.8 us
    all_to_all x3, starting transfers between devices, send_forth(): lax.all_to_all(buffer, ('sec', 'blk'), split_axis=0, concat_axis=0, tiled...  35.5 us
    ppermute x13, starting transfers between devices, with_halo(): before = lax.ppermute(last, axis, up)  32.2 us
    unnamed x74, local copies, waits for them, and re-layouts  25 us
    all_to_all x3, waiting for transfers between devices, local(): lax.all_to_all(reply_tiles.reshape(devices, slots_each, 3, tile_size), ('...  18.4 us
    ppermute x6, starting transfers between devices, plane_sides(): lax.ppermute(lax.slice_in_dim(plane, length - 1, length, axis=dim), axis,...  18 us
  transfers between devices with their start and end apart: 45, of which 12 were waited for; matrix products, arithmetic and copies ran while one was open for 21% of the time, Pallas kernels for 0%

profile of v1, /device:TPU:32, one launch (start us, length us, event | category | flops | bytes accessed | tf_op | source)
XLA Modules:
  0.0 480.1 jit_solution(12328001899483011513)
XLA Ops:
  0.7 4.0 copy.741
  9.3 3.9 collective-permute-start.1
  14.5 10.7 %all-to-all-start = ((s32[128,1,2]{2,1,0:T(1,128)}), s32[128,1,2]{2,1,0:T(1,128)S(1)}, u32[]{:S(2)}, u32[]{:S(2)}) async-start(s32[128,1,2]{2,1,0:T(1,128)} %bitcast.13), calls=%async_computation | async-start | bytes 131072 | tf_op jit(solution)/shard_map/all_to_all | solution.py:103
  27.3 7.7 %collective-permute-start.13 = (f32[3,64]{1,0:T(4,128)S(1)}, f32[3,64]{1,0:T(4,128)S(1)}, u32[]{:S(2)}, u32[]{:S(2)}) collective-permute-start(f32[3,64]{1,0:T(4,128)S(1)} %get-tuple-element.104), channel_id=1, source_target_pairs={{1,0},{2,1},{3,2},{4,3},{5,4},{6,5},{7,6},{8,7},{9,8},{10,9},{11,1... | collective-permute-start | bytes 2312 | tf_op jit(solution)/shard_map/ppermute | solution.py:23
  35.1 8.3 %fusion.177 = (f32[5,32,16,255]{3,0,2,1:T(8,128)}, f32[5,32,16,255]{3,0,2,1:T(8,128)}) fusion(f32[5,32,16,256]{3,0,2,1:T(8,128)} %copy-done.1), kind=kLoop, calls=%fused_computation.259 | loop fusion | bytes 10444800 | tf_op jit(solution)/shard_map/slice | solution.py:35
  51.7 5.5 %all-to-all-start.1 = ((f32[128,1,384]{2,1,0:T(1,128)}), f32[128,1,384]{2,1,0:T(1,128)S(1)}, u32[]{:S(2)}, u32[]{:S(2)}) async-start(f32[128,1,384]{2,1,0:T(1,128)} %reshape.469), calls=%async_computation.1 | async-start | bytes 393216 | tf_op jit(solution)/shard_map/all_to_all | solution.py:184
  64.1 3.9 collective-permute-start.3
  68.1 7.1 %fusion.14 = f32[32,16,256,5]{2,3,1,0:T(8,128)} fusion(f32[5,1,16,256]{3,0,2,1:T(8,128)} %collective-permute-done, f32[5,32,16,256]{3,0,2,1:T(8,128)S(1)} %copy-done.2, f32[5,1,16,256]{3,0,2,1:T(8,128)} %collective-permute-done.1, f32[5,5]{1,0:T(8,128)S(1)} %copy-done.9), kind=kOutput, calls=%fused_computation.30 | convolution fusion | flops 41943040 | bytes 5406820 | tf_op jit(solution)/shard_map/cd,dxyz->cxyz/dot_general | solution.py:40
  79.8 5.6 %fusion.30 = f32[3,8,64]{2,0,1:T(4,128)S(1)} fusion(f32[8,16,64,64]{3,2,1,0:T(8,128)} %param.22, f32[8,16,3,64]{3,1,2,0:T(8,128)S(1)} %fusion.48, f32[8]{0:T(128)} %compare_convert_fusion), kind=kOutput, calls=%fused_computation.60 | convolution fusion | flops 18875904 | bytes 2201632 | tf_op jit(solution)/shard_map/rkqn,rkcn->rcq/dot_general | solution.py:195
  92.9 3.3 collective-permute-start.11
  98.1 24.3 %fusion.4 = f32[5,32,16,256]{3,0,2,1:T(8,128)} fusion(f32[5,32,16,256]{3,0,2,1:T(8,128)} %copy-done.1, f32[32,16,256,5]{2,3,1,0:T(8,128)} %fusion.14, f32[5,32,16,255]{3,0,2,1:T(8,128)} %get-tuple-element.57, f32[5,32,16,255]{3,0,2,1:T(8,128)} %get-tuple-element.56, f32[5,1,16,256]{3,0,2,1:T(8,128)} %collective-permute-done, ...), kind=kOutput, calls=%fused_computation.19 | convolution fusion | flops 52428800 | bytes 16908388 | tf_op jit(solution)/shard_map/cd,dxyz->cxyz/dot_general | solution.py:43
  129.5 8.3 %fusion.175 = (f32[5,32,16,255]{3,0,2,1:T(8,128)}, f32[5,32,16,255]{3,0,2,1:T(8,128)}) fusion(f32[5,32,16,256]{3,0,2,1:T(8,128)} %fusion.4), kind=kLoop, calls=%fused_computation.257 | loop fusion | bytes 10444800 | tf_op jit(solution)/shard_map/slice | solution.py:35
  139.2 3.8 collective-permute-start.7
  143.1 5.7 %fusion.8 = f32[32,16,256,5]{2,3,1,0:T(8,128)} fusion(f32[5,1,16,256]{3,0,2,1:T(8,128)S(1)} %collective-permute-done.4, f32[5,32,16,256]{3,0,2,1:T(8,128)S(1)} %copy-done, f32[5,1,16,256]{3,0,2,1:T(8,128)S(1)} %collective-permute-done.5, f32[5,5]{1,0:T(8,128)S(1)} %copy-done.11), kind=kOutput, calls=%fused_computation.24 | convolution fusion | flops 41943040 | bytes 5406820 | tf_op jit(solution)/shard_map/cd,dxyz->cxyz/dot_general | solution.py:40
  149.6 27.5 %fusion.2 = f32[5,32,16,256]{3,0,2,1:T(8,128)} fusion(f32[32,16,256,5]{2,3,1,0:T(8,128)} %fusion.8, f32[5,32,16,256]{3,0,2,1:T(8,128)} %fusion.4, f32[5,32,16,255]{3,0,2,1:T(8,128)} %get-tuple-element.53, f32[5,32,16,255]{3,0,2,1:T(8,128)} %get-tuple-element.52, f32[5,1,16,256]{3,0,2,1:T(8,128)S(1)} %collective-permute-done.4, ...), kind=kOutput, calls=%fused_computation.15 | convolution fusion | flops 58982400 | bytes 16744548 | tf_op jit(solution)/shard_map/cd,dxyz->cxyz/dot_general | solution.py:43
  180.0 4.3 convolution_multiply_fusion.2
  186.1 17.7 %all-to-all-start.2 = ((f32[128,1,384]{2,1,0:T(1,128)}), f32[128,1,384]{2,1,0:T(1,128)S(1)}, u32[]{:S(2)}, u32[]{:S(2)}) async-start(f32[128,1,384]{2,1,0:T(1,128)} %reshape.471), calls=%async_computation.2 | async-start | bytes 393216 | tf_op jit(solution)/shard_map/all_to_all | solution.py:119
  203.9 5.1 %convolution_bitcast_fusion.8 = f32[16,3,64]{2,1,0:T(4,128)S(1)} fusion(f32[16,8,64,64]{3,2,1,0:T(8,128)} %param.28, f32[16,8,3,64]{3,1,2,0:T(8,128)S(1)} %fusion.89), kind=kOutput, calls=%fused_computation.48 | convolution fusion | flops 18874368 | bytes 2207744 | tf_op jit(solution)/shard_map/ibmn,ibcn->cim/dot_general | solution.py:145
  217.4 7.9 %collective-permute-start.15 = (f32[3,64]{1,0:T(4,128)S(1)}, f32[3,64]{1,0:T(4,128)S(1)}, u32[]{:S(2)}, u32[]{:S(2)}) collective-permute-start(f32[3,64]{1,0:T(4,128)S(1)} %get-tuple-element.102), channel_id=1, source_target_pairs={{1,0},{2,1},{3,2},{4,3},{5,4},{6,5},{7,6},{8,7},{9,8},{10,9},{11,1... | collective-permute-start | bytes 2312 | tf_op jit(solution)/shard_map/ppermute | solution.py:23
  227.1 5.1 %convolution_bitcast_fusion.7 = f32[16,3,64]{2,1,0:T(4,128)S(1)} fusion(f32[16,8,64,64]{3,2,1,0:T(8,128)} %param.28, f32[16,8,3,64]{3,1,2,0:T(8,128)S(1)} %fusion.87), kind=kOutput, calls=%fused_computation.47 | convolution fusion | flops 18874368 | bytes 2207744 | tf_op jit(solution)/shard_map/ibmn,ibcn->cim/dot_general | solution.py:145
  234.3 7.9 %collective-permute-start.17 = (f32[3,64]{1,0:T(4,128)S(1)}, f32[3,64]{1,0:T(4,128)S(1)}, u32[]{:S(2)}, u32[]{:S(2)}) collective-permute-start(f32[3,64]{1,0:T(4,128)S(1)} %get-tuple-element.100), channel_id=1, source_target_pairs={{1,0},{2,1},{3,2},{4,3},{5,4},{6,5},{7,6},{8,7},{9,8},{10,9},{11,1... | collective-permute-start | bytes 2312 | tf_op jit(solution)/shard_map/ppermute | solution.py:23
  244.0 5.1 %convolution_bitcast_fusion.6 = f32[16,3,64]{2,1,0:T(4,128)S(1)} fusion(f32[16,8,64,64]{3,2,1,0:T(8,128)} %param.28, f32[16,8,3,64]{3,1,2,0:T(8,128)S(1)} %fusion.85), kind=kOutput, calls=%fused_computation.46 | convolution fusion | flops 18874368 | bytes 2207744 | tf_op jit(solution)/shard_map/ibmn,ibcn->cim/dot_general | solution.py:145
  251.3 7.9 %collective-permute-start.23 = (f32[3,64]{1,0:T(4,128)S(1)}, f32[3,64]{1,0:T(4,128)S(1)}, u32[]{:S(2)}, u32[]{:S(2)}) collective-permute-start(f32[3,64]{1,0:T(4,128)S(1)} %get-tuple-element.98), channel_id=1, source_target_pairs={{1,0},{2,1},{3,2},{4,3},{5,4},{6,5},{7,6},{8,7},{9,8},{10,9},{11,1... | collective-permute-start | bytes 2312 | tf_op jit(solution)/shard_map/ppermute | solution.py:23
  260.8 3.9 all-to-all-start.3
  265.2 9.2 %all-to-all-done.3 = f32[128,1,384]{2,1,0:T(1,128)S(1)} async-done(((f32[128,1,384]{2,1,0:T(1,128)}), f32[128,1,384]{2,1,0:T(1,128)S(1)}, u32[]{:S(2)}, u32[]{:S(2)}) %all-to-all-start.3) | async-done | bytes 196640 | tf_op jit(solution)/shard_map/all_to_all | solution.py:184
  276.1 5.6 %fusion.28 = f32[3,8,64]{2,0,1:T(4,128)S(1)} fusion(f32[8,16,64,64]{3,2,1,0:T(8,128)} %param.22, f32[8,16,3,64]{3,1,2,0:T(8,128)S(1)} %fusion.46, f32[8]{0:T(128)S(1)} %copy-done.16), kind=kOutput, calls=%fused_computation.57 | convolution fusion | flops 18875904 | bytes 2201632 | tf_op jit(solution)/shard_map/rkqn,rkcn->rcq/dot_general | solution.py:195
  293.6 4.3 convolution_multiply_fusion.1
  299.7 8.9 %all-to-all-start.4 = ((f32[128,1,384]{2,1,0:T(1,128)}), f32[128,1,384]{2,1,0:T(1,128)S(1)}, u32[]{:S(2)}, u32[]{:S(2)}) async-start(f32[128,1,384]{2,1,0:T(1,128)} %reshape.475), calls=%async_computation.4 | async-start | bytes 393216 | tf_op jit(solution)/shard_map/all_to_all | solution.py:119
  308.6 5.1 %convolution_bitcast_fusion.5 = f32[16,3,64]{2,1,0:T(4,128)S(1)} fusion(f32[16,8,64,64]{3,2,1,0:T(8,128)} %param.28, f32[16,8,3,64]{3,1,2,0:T(8,128)S(1)} %fusion.83), kind=kOutput, calls=%fused_computation.45 | convolution fusion | flops 18874368 | bytes 2207744 | tf_op jit(solution)/shard_map/ibmn,ibcn->cim/dot_general | solution.py:145
  313.7 4.6 all-to-all-done.4
  322.1 7.9 %collective-permute-start.25 = (f32[3,64]{1,0:T(4,128)S(1)}, f32[3,64]{1,0:T(4,128)S(1)}, u32[]{:S(2)}, u32[]{:S(2)}) collective-permute-start(f32[3,64]{1,0:T(4,128)S(1)} %get-tuple-element.96), channel_id=1, source_target_pairs={{1,0},{2,1},{3,2},{4,3},{5,4},{6,5},{7,6},{8,7},{9,8},{10,9},{11,1... | collective-permute-start | bytes 2312 | tf_op jit(solution)/shard_map/ppermute | solution.py:23
  331.8 5.7 %convolution_bitcast_fusion.4 = f32[16,3,64]{2,1,0:T(4,128)S(1)} fusion(f32[16,8,64,64]{3,2,1,0:T(8,128)} %param.28, f32[16,8,3,64]{3,1,2,0:T(8,128)S(1)} %fusion.81), kind=kOutput, calls=%fused_computation.44 | convolution fusion | flops 18874368 | bytes 2207744 | tf_op jit(solution)/shard_map/ibmn,ibcn->cim/dot_general | solution.py:145
  339.6 7.9 %collective-permute-start.27 = (f32[3,64]{1,0:T(4,128)S(1)}, f32[3,64]{1,0:T(4,128)S(1)}, u32[]{:S(2)}, u32[]{:S(2)}) collective-permute-start(f32[3,64]{1,0:T(4,128)S(1)} %get-tuple-element.94), channel_id=1, source_target_pairs={{1,0},{2,1},{3,2},{4,3},{5,4},{6,5},{7,6},{8,7},{9,8},{10,9},{11,1... | collective-permute-start | bytes 2312 | tf_op jit(solution)/shard_map/ppermute | solution.py:23
  349.3 5.1 %convolution_bitcast_fusion.3 = f32[16,3,64]{2,1,0:T(4,128)S(1)} fusion(f32[16,8,64,64]{3,2,1,0:T(8,128)} %param.28, f32[16,8,3,64]{3,1,2,0:T(8,128)S(1)} %fusion.79), kind=kOutput, calls=%fused_computation.43 | convolution fusion | flops 18874368 | bytes 2207744 | tf_op jit(solution)/shard_map/ibmn,ibcn->cim/dot_general | solution.py:145
  356.6 7.9 %collective-permute-start.33 = (f32[3,64]{1,0:T(4,128)S(1)}, f32[3,64]{1,0:T(4,128)S(1)}, u32[]{:S(2)}, u32[]{:S(2)}) collective-permute-start(f32[3,64]{1,0:T(4,128)S(1)} %get-tuple-element.92), channel_id=1, source_target_pairs={{1,0},{2,1},{3,2},{4,3},{5,4},{6,5},{7,6},{8,7},{9,8},{10,9},{11,1... | collective-permute-start | bytes 2312 | tf_op jit(solution)/shard_map/ppermute | solution.py:23
  366.1 3.5 all-to-all-start.5
  370.2 9.2 %all-to-all-done.5 = f32[128,1,384]{2,1,0:T(1,128)S(1)} async-done(((f32[128,1,384]{2,1,0:T(1,128)}), f32[128,1,384]{2,1,0:T(1,128)S(1)}, u32[]{:S(2)}, u32[]{:S(2)}) %all-to-all-start.5) | async-done | bytes 196640 | tf_op jit(solution)/shard_map/all_to_all | solution.py:184
  381.2 5.6 %fusion.26 = f32[3,8,64]{2,0,1:T(4,128)S(1)} fusion(f32[8,16,64,64]{3,2,1,0:T(8,128)} %param.22, f32[8,16,3,64]{3,1,2,0:T(8,128)S(1)} %fusion.44, f32[8]{0:T(128)S(1)} %copy-done.16), kind=kOutput, calls=%fused_computation.54 | convolution fusion | flops 18875904 | bytes 2201632 | tf_op jit(solution)/shard_map/rkqn,rkcn->rcq/dot_general | solution.py:195
  398.8 4.3 convolution_multiply_fusion
  404.8 8.9 %all-to-all-start.6 = ((f32[128,1,384]{2,1,0:T(1,128)}), f32[128,1,384]{2,1,0:T(1,128)S(1)}, u32[]{:S(2)}, u32[]{:S(2)}) async-start(f32[128,1,384]{2,1,0:T(1,128)} %reshape.479), calls=%async_computation.6 | async-start | bytes 393216 | tf_op jit(solution)/shard_map/all_to_all | solution.py:119
  413.7 5.1 %convolution_bitcast_fusion.2 = f32[16,3,64]{2,1,0:T(4,128)S(1)} fusion(f32[16,8,64,64]{3,2,1,0:T(8,128)} %param.28, f32[16,8,3,64]{3,1,2,0:T(8,128)S(1)} %fusion.77), kind=kOutput, calls=%fused_computation.42 | convolution fusion | flops 18874368 | bytes 2207744 | tf_op jit(solution)/shard_map/ibmn,ibcn->cim/dot_general | solution.py:145
  418.9 4.6 all-to-all-done.6
  427.3 7.9 %collective-permute-start.35 = (f32[3,64]{1,0:T(4,128)S(1)}, f32[3,64]{1,0:T(4,128)S(1)}, u32[]{:S(2)}, u32[]{:S(2)}) collective-permute-start(f32[3,64]{1,0:T(4,128)S(1)} %get-tuple-element.90), channel_id=1, source_target_pairs={{1,0},{2,1},{3,2},{4,3},{5,4},{6,5},{7,6},{8,7},{9,8},{10,9},{11,1... | collective-permute-start | bytes 2312 | tf_op jit(solution)/shard_map/ppermute | solution.py:23
  436.9 5.1 %convolution_bitcast_fusion.1 = f32[16,3,64]{2,1,0:T(4,128)S(1)} fusion(f32[16,8,64,64]{3,2,1,0:T(8,128)} %param.28, f32[16,8,3,64]{3,1,2,0:T(8,128)S(1)} %fusion.75), kind=kOutput, calls=%fused_computation.41 | convolution fusion | flops 18874368 | bytes 2207744 | tf_op jit(solution)/shard_map/ibmn,ibcn->cim/dot_general | solution.py:145
  444.2 8.1 %collective-permute-start.37 = (f32[3,64]{1,0:T(4,128)S(1)}, f32[3,64]{1,0:T(4,128)S(1)}, u32[]{:S(2)}, u32[]{:S(2)}) collective-permute-start(f32[3,64]{1,0:T(4,128)S(1)} %get-tuple-element.88), channel_id=1, source_target_pairs={{1,0},{2,1},{3,2},{4,3},{5,4},{6,5},{7,6},{8,7},{9,8},{10,9},{11,1... | collective-permute-start | bytes 2312 | tf_op jit(solution)/shard_map/ppermute | solution.py:23
  454.2 14.9 %dynamic_update_slice.3 = f32[5,32,16,256]{3,0,2,1:T(8,128)} dynamic-update-slice(f32[5,32,16,256]{3,0,2,1:T(8,128)} %fusion.2, f32[5,32,16,2]{3,0,2,1:T(8,128)S(1)} %copy.805, s32[]{:T(128)} %constant.79.clone.1, s32[]{:T(128)} %constant.79.clone.1, s32[]{:T(128)} %constant.79.clone.1, s32[]{:T(128)} %constant.79.clone.1) | dynamic-update-slice | bytes 40964 | tf_op jit(solution)/shard_map/dynamic_update_slice | solution.py:212
  469.0 4.5 copy.818
  474.0 5.1 %convolution_bitcast_fusion = f32[16,3,64]{2,1,0:T(4,128)S(1)} fusion(f32[16,8,64,64]{3,2,1,0:T(8,128)} %param.28, f32[16,8,3,64]{3,1,2,0:T(8,128)S(1)} %fusion.73), kind=kOutput, calls=%fused_computation.40 | convolution fusion | flops 18874368 | bytes 2207744 | tf_op jit(solution)/shard_map/ibmn,ibcn->cim/dot_general | solution.py:145
  (322 shorter events, 123.3 us)
Async XLA Ops:
  7.4 53.6 %collective-permute-start = (f32[5,1,16,256]{3,0,2,1:T(8,128)}, f32[5,1,16,256]{3,0,2,1:T(8,128)}, u32[]{:S(2)}, u32[]{:S(2)}) collective-permute-start(f32[5,1,16,256]{3,0,2,1:T(8,128)} %get-tuple-element.59), channel_id=1, source_target_pairs={{32,0},{64,32},{96,64},{33,1},{65,33},{97,65},{34,2},{66,34},{98,6... | collective-permute-start | bytes 245768 | tf_op jit(solution)/shard_map/ppermute | solution.py:23
  9.3 48.0 %collective-permute-start.1 = (f32[5,1,16,256]{3,0,2,1:T(8,128)}, f32[5,1,16,256]{3,0,2,1:T(8,128)}, u32[]{:S(2)}, u32[]{:S(2)}) collective-permute-start(f32[5,1,16,256]{3,0,2,1:T(8,128)} %get-tuple-element.58), channel_id=1, source_target_pairs={{0,32},{32,64},{64,96},{1,33},{33,65},{65,97},{2,34},{34,66},{66,9... | collective-permute-start | bytes 245768 | tf_op jit(solution)/shard_map/ppermute | solution.py:22
  14.5 33.3 %all-to-all-start = ((s32[128,1,2]{2,1,0:T(1,128)}), s32[128,1,2]{2,1,0:T(1,128)S(1)}, u32[]{:S(2)}, u32[]{:S(2)}) async-start(s32[128,1,2]{2,1,0:T(1,128)} %bitcast.13), calls=%async_computation | async-start | bytes 131072 | tf_op jit(solution)/shard_map/all_to_all | solution.py:103
  25.3 22.1 %collective-permute-start.12 = (f32[3,64]{1,0:T(4,128)S(1)}, f32[3,64]{1,0:T(4,128)S(1)}, u32[]{:S(2)}, u32[]{:S(2)}) collective-permute-start(f32[3,64]{1,0:T(4,128)S(1)} %get-tuple-element.105), channel_id=1, source_target_pairs={{0,1},{1,2},{2,3},{3,4},{4,5},{5,6},{6,7},{7,8},{8,9},{9,10},{10,1... | collective-permute-start | bytes 2312 | tf_op jit(solution)/shard_map/ppermute | solution.py:22
  27.3 20.0 %collective-permute-start.13 = (f32[3,64]{1,0:T(4,128)S(1)}, f32[3,64]{1,0:T(4,128)S(1)}, u32[]{:S(2)}, u32[]{:S(2)}) collective-permute-start(f32[3,64]{1,0:T(4,128)S(1)} %get-tuple-element.104), channel_id=1, source_target_pairs={{1,0},{2,1},{3,2},{4,3},{5,4},{6,5},{7,6},{8,7},{9,8},{10,9},{11,1... | collective-permute-start | bytes 2312 | tf_op jit(solution)/shard_map/ppermute | solution.py:23
  51.7 23.5 %all-to-all-start.1 = ((f32[128,1,384]{2,1,0:T(1,128)}), f32[128,1,384]{2,1,0:T(1,128)S(1)}, u32[]{:S(2)}, u32[]{:S(2)}) async-start(f32[128,1,384]{2,1,0:T(1,128)} %reshape.469), calls=%async_computation.1 | async-start | bytes 393216 | tf_op jit(solution)/shard_map/all_to_all | solution.py:184
  62.8 35.3 %collective-permute-start.2 = (f32[5,34,1,256]{3,0,2,1:T(8,128)}, f32[5,34,1,256]{3,0,2,1:T(8,128)}, u32[]{:S(2)}, u32[]{:S(2)}) collective-permute-start(f32[5,34,1,256]{3,0,2,1:T(8,128)} %get-tuple-element.51), channel_id=1, source_target_pairs={{1,0},{2,1},{3,2},{4,3},{5,4},{6,5},{7,6},{8,7},{9,8},{10,9},{11,1... | collective-permute-start | bytes 522248 | tf_op jit(solution)/shard_map/ppermute | solution.py:23
  64.1 34.0 %collective-permute-start.3 = (f32[5,34,1,256]{3,0,2,1:T(8,128)}, f32[5,34,1,256]{3,0,2,1:T(8,128)}, u32[]{:S(2)}, u32[]{:S(2)}) collective-permute-start(f32[5,34,1,256]{3,0,2,1:T(8,128)} %get-tuple-element.50), channel_id=1, source_target_pairs={{0,1},{1,2},{2,3},{3,4},{4,5},{5,6},{6,7},{7,8},{8,9},{9,10},{10,1... | collective-permute-start | bytes 522248 | tf_op jit(solution)/shard_map/ppermute | solution.py:22
  85.8 7.2 %collective-permute-start.8 = (f32[3,1,16]{1,2,0:T(8,128)S(1)}, f32[3,1,16]{1,2,0:T(8,128)S(1)}, u32[]{:S(2)}, u32[]{:S(2)}) collective-permute-start(f32[3,1,16]{1,2,0:T(8,128)S(1)} %get-tuple-element.81), channel_id=1, source_target_pairs={{32,0},{64,32},{96,64},{33,1},{65,33},{97,65},{34,2},{66,34},{98,6... | collective-permute-start | bytes 584 | tf_op jit(solution)/shard_map/ppermute | solution.py:60
  88.6 7.6 %collective-permute-start.9 = (f32[3,1,16]{1,2,0:T(8,128)S(1)}, f32[3,1,16]{1,2,0:T(8,128)S(1)}, u32[]{:S(2)}, u32[]{:S(2)}) collective-permute-start(f32[3,1,16]{1,2,0:T(8,128)S(1)} %get-tuple-element.80), channel_id=1, source_target_pairs={{0,32},{32,64},{64,96},{1,33},{33,65},{65,97},{2,34},{34,66},{66,9... | collective-permute-start | bytes 584 | tf_op jit(solution)/shard_map/ppermute | solution.py:59
  91.6 5.6 %collective-permute-start.10 = (f32[3,32,1]{1,2,0:T(1,128)S(1)}, f32[3,32,1]{1,2,0:T(1,128)S(1)}, u32[]{:S(2)}, u32[]{:S(2)}) collective-permute-start(f32[3,32,1]{1,2,0:T(1,128)S(1)} %get-tuple-element.85), channel_id=1, source_target_pairs={{1,0},{2,1},{3,2},{4,3},{5,4},{6,5},{7,6},{8,7},{9,8},{10,9},{11,1... | collective-permute-start | bytes 1160 | tf_op jit(solution)/shard_map/ppermute | solution.py:60
  92.9 4.3 collective-permute-start.11
  123.4 14.5 %collective-permute-start.4 = (f32[5,1,16,256]{3,0,2,1:T(8,128)S(1)}, f32[5,1,16,256]{3,0,2,1:T(8,128)S(1)}, u32[]{:S(2)}, u32[]{:S(2)}) collective-permute-start(f32[5,1,16,256]{3,0,2,1:T(8,128)S(1)} %get-tuple-element.55), channel_id=1, source_target_pairs={{32,0},{64,32},{96,64},{33,1},{65,33},{97,65},{34,2},{66,34},{98,6... | collective-permute-start | bytes 245768 | tf_op jit(solution)/shard_map/ppermute | solution.py:23
  126.3 11.6 %collective-permute-start.5 = (f32[5,1,16,256]{3,0,2,1:T(8,128)S(1)}, f32[5,1,16,256]{3,0,2,1:T(8,128)S(1)}, u32[]{:S(2)}, u32[]{:S(2)}) collective-permute-start(f32[5,1,16,256]{3,0,2,1:T(8,128)S(1)} %get-tuple-element.54), channel_id=1, source_target_pairs={{0,32},{32,64},{64,96},{1,33},{33,65},{65,97},{2,34},{34,66},{66,9... | collective-permute-start | bytes 245768 | tf_op jit(solution)/shard_map/ppermute | solution.py:22
  137.9 10.9 %collective-permute-start.6 = (f32[5,34,1,256]{3,0,2,1:T(8,128)S(1)}, f32[5,34,1,256]{3,0,2,1:T(8,128)S(1)}, u32[]{:S(2)}, u32[]{:S(2)}) collective-permute-start(f32[5,34,1,256]{3,0,2,1:T(8,128)S(1)} %get-tuple-element.49), channel_id=1, source_target_pairs={{1,0},{2,1},{3,2},{4,3},{5,4},{6,5},{7,6},{8,7},{9,8},{10,9},{11,1... | collective-permute-start | bytes 522248 | tf_op jit(solution)/shard_map/ppermute | solution.py:23
  139.2 9.6 %collective-permute-start.7 = (f32[5,34,1,256]{3,0,2,1:T(8,128)S(1)}, f32[5,34,1,256]{3,0,2,1:T(8,128)S(1)}, u32[]{:S(2)}, u32[]{:S(2)}) collective-permute-start(f32[5,34,1,256]{3,0,2,1:T(8,128)S(1)} %get-tuple-element.48), channel_id=1, source_target_pairs={{0,1},{1,2},{2,3},{3,4},{4,5},{5,6},{6,7},{7,8},{8,9},{9,10},{10,1... | collective-permute-start | bytes 522248 | tf_op jit(solution)/shard_map/ppermute | solution.py:22
  186.1 27.5 %all-to-all-start.2 = ((f32[128,1,384]{2,1,0:T(1,128)}), f32[128,1,384]{2,1,0:T(1,128)S(1)}, u32[]{:S(2)}, u32[]{:S(2)}) async-start(f32[128,1,384]{2,1,0:T(1,128)} %reshape.471), calls=%async_computation.2 | async-start | bytes 393216 | tf_op jit(solution)/shard_map/all_to_all | solution.py:119
  215.5 9.8 %collective-permute-start.14 = (f32[3,64]{1,0:T(4,128)S(1)}, f32[3,64]{1,0:T(4,128)S(1)}, u32[]{:S(2)}, u32[]{:S(2)}) collective-permute-start(f32[3,64]{1,0:T(4,128)S(1)} %get-tuple-element.103), channel_id=1, source_target_pairs={{0,1},{1,2},{2,3},{3,4},{4,5},{5,6},{6,7},{7,8},{8,9},{9,10},{10,1... | collective-permute-start | bytes 2312 | tf_op jit(solution)/shard_map/ppermute | solution.py:22
  217.4 9.2 %collective-permute-start.15 = (f32[3,64]{1,0:T(4,128)S(1)}, f32[3,64]{1,0:T(4,128)S(1)}, u32[]{:S(2)}, u32[]{:S(2)}) collective-permute-start(f32[3,64]{1,0:T(4,128)S(1)} %get-tuple-element.102), channel_id=1, source_target_pairs={{1,0},{2,1},{3,2},{4,3},{5,4},{6,5},{7,6},{8,7},{9,8},{10,9},{11,1... | collective-permute-start | bytes 2312 | tf_op jit(solution)/shard_map/ppermute | solution.py:23
  227.1 32.1 %copy-start.18 = (s32[128,2]{0,1:T(2,128)S(1)}, s32[128,2]{0,1:T(2,128)}, u32[]{:S(2)}) copy-start(s32[128,2]{0,1:T(2,128)} %copy-done.17) | copy-start | bytes 3076
  232.4 9.8 %collective-permute-start.16 = (f32[3,64]{1,0:T(4,128)S(1)}, f32[3,64]{1,0:T(4,128)S(1)}, u32[]{:S(2)}, u32[]{:S(2)}) collective-permute-start(f32[3,64]{1,0:T(4,128)S(1)} %get-tuple-element.101), channel_id=1, source_target_pairs={{0,1},{1,2},{2,3},{3,4},{4,5},{5,6},{6,7},{7,8},{8,9},{9,10},{10,1... | collective-permute-start | bytes 2312 | tf_op jit(solution)/shard_map/ppermute | solution.py:22
  234.3 9.2 %collective-permute-start.17 = (f32[3,64]{1,0:T(4,128)S(1)}, f32[3,64]{1,0:T(4,128)S(1)}, u32[]{:S(2)}, u32[]{:S(2)}) collective-permute-start(f32[3,64]{1,0:T(4,128)S(1)} %get-tuple-element.100), channel_id=1, source_target_pairs={{1,0},{2,1},{3,2},{4,3},{5,4},{6,5},{7,6},{8,7},{9,8},{10,9},{11,1... | collective-permute-start | bytes 2312 | tf_op jit(solution)/shard_map/ppermute | solution.py:23
  244.0 31.9 %copy-start.13 = (s32[8,16]{1,0:T(8,128)S(1)}, s32[8,16]{1,0:T(8,128)}, u32[]{:S(2)}) copy-start(s32[8,16]{1,0:T(8,128)} %multiply_add_fusion.1) | copy-start | bytes 1540
  249.4 15.4 %collective-permute-start.22 = (f32[3,64]{1,0:T(4,128)S(1)}, f32[3,64]{1,0:T(4,128)S(1)}, u32[]{:S(2)}, u32[]{:S(2)}) collective-permute-start(f32[3,64]{1,0:T(4,128)S(1)} %get-tuple-element.99), channel_id=1, source_target_pairs={{0,1},{1,2},{2,3},{3,4},{4,5},{5,6},{6,7},{7,8},{8,9},{9,10},{10,1... | collective-permute-start | bytes 2312 | tf_op jit(solution)/shard_map/ppermute | solution.py:22
  251.3 13.5 %collective-permute-start.23 = (f32[3,64]{1,0:T(4,128)S(1)}, f32[3,64]{1,0:T(4,128)S(1)}, u32[]{:S(2)}, u32[]{:S(2)}) collective-permute-start(f32[3,64]{1,0:T(4,128)S(1)} %get-tuple-element.98), channel_id=1, source_target_pairs={{1,0},{2,1},{3,2},{4,3},{5,4},{6,5},{7,6},{8,7},{9,8},{10,9},{11,1... | collective-permute-start | bytes 2312 | tf_op jit(solution)/shard_map/ppermute | solution.py:23
  260.8 31.6 %copy-start.12 = (f32[5,5]{1,0:T(8,128)S(1)}, f32[5,5]{1,0:T(8,128)}, u32[]{:S(2)}) copy-start(f32[5,5]{1,0:T(8,128)} %param.19) | copy-start | bytes 304
  260.8 13.6 %all-to-all-start.3 = ((f32[128,1,384]{2,1,0:T(1,128)}), f32[128,1,384]{2,1,0:T(1,128)S(1)}, u32[]{:S(2)}, u32[]{:S(2)}) async-start(f32[128,1,384]{2,1,0:T(1,128)} %reshape.473), calls=%async_computation.3 | async-start | bytes 393216 | tf_op jit(solution)/shard_map/all_to_all | solution.py:184
  282.1 10.2 %collective-permute-start.18 = (f32[3,1,16]{1,2,0:T(8,128)S(1)}, f32[3,1,16]{1,2,0:T(8,128)S(1)}, u32[]{:S(2)}, u32[]{:S(2)}) collective-permute-start(f32[3,1,16]{1,2,0:T(8,128)S(1)} %get-tuple-element.73), channel_id=1, source_target_pairs={{32,0},{64,32},{96,64},{33,1},{65,33},{97,65},{34,2},{66,34},{98,6... | collective-permute-start | bytes 584 | tf_op jit(solution)/shard_map/ppermute | solution.py:60
  285.2 7.1 %collective-permute-start.19 = (f32[3,1,16]{1,2,0:T(8,128)S(1)}, f32[3,1,16]{1,2,0:T(8,128)S(1)}, u32[]{:S(2)}, u32[]{:S(2)}) collective-permute-start(f32[3,1,16]{1,2,0:T(8,128)S(1)} %get-tuple-element.72), channel_id=1, source_target_pairs={{0,32},{32,64},{64,96},{1,33},{33,65},{65,97},{2,34},{34,66},{66,9... | collective-permute-start | bytes 584 | tf_op jit(solution)/shard_map/ppermute | solution.py:59
  288.0 4.7 collective-permute-start.20
  289.3 3.8 collective-permute-start.21
  299.7 18.6 %all-to-all-start.4 = ((f32[128,1,384]{2,1,0:T(1,128)}), f32[128,1,384]{2,1,0:T(1,128)S(1)}, u32[]{:S(2)}, u32[]{:S(2)}) async-start(f32[128,1,384]{2,1,0:T(1,128)} %reshape.475), calls=%async_computation.4 | async-start | bytes 393216 | tf_op jit(solution)/shard_map/all_to_all | solution.py:119
  320.2 10.0 %collective-permute-start.24 = (f32[3,64]{1,0:T(4,128)S(1)}, f32[3,64]{1,0:T(4,128)S(1)}, u32[]{:S(2)}, u32[]{:S(2)}) collective-permute-start(f32[3,64]{1,0:T(4,128)S(1)} %get-tuple-element.97), channel_id=1, source_target_pairs={{0,1},{1,2},{2,3},{3,4},{4,5},{5,6},{6,7},{7,8},{8,9},{9,10},{10,1... | collective-permute-start | bytes 2312 | tf_op jit(solution)/shard_map/ppermute | solution.py:22
  322.1 9.2 %collective-permute-start.25 = (f32[3,64]{1,0:T(4,128)S(1)}, f32[3,64]{1,0:T(4,128)S(1)}, u32[]{:S(2)}, u32[]{:S(2)}) collective-permute-start(f32[3,64]{1,0:T(4,128)S(1)} %get-tuple-element.96), channel_id=1, source_target_pairs={{1,0},{2,1},{3,2},{4,3},{5,4},{6,5},{7,6},{8,7},{9,8},{10,9},{11,1... | collective-permute-start | bytes 2312 | tf_op jit(solution)/shard_map/ppermute | solution.py:23
  337.7 10.7 %collective-permute-start.26 = (f32[3,64]{1,0:T(4,128)S(1)}, f32[3,64]{1,0:T(4,128)S(1)}, u32[]{:S(2)}, u32[]{:S(2)}) collective-permute-start(f32[3,64]{1,0:T(4,128)S(1)} %get-tuple-element.95), channel_id=1, source_target_pairs={{0,1},{1,2},{2,3},{3,4},{4,5},{5,6},{6,7},{7,8},{8,9},{9,10},{10,1... | collective-permute-start | bytes 2312 | tf_op jit(solution)/shard_map/ppermute | solution.py:22
  339.6 9.2 %collective-permute-start.27 = (f32[3,64]{1,0:T(4,128)S(1)}, f32[3,64]{1,0:T(4,128)S(1)}, u32[]{:S(2)}, u32[]{:S(2)}) collective-permute-start(f32[3,64]{1,0:T(4,128)S(1)} %get-tuple-element.94), channel_id=1, source_target_pairs={{1,0},{2,1},{3,2},{4,3},{5,4},{6,5},{7,6},{8,7},{9,8},{10,9},{11,1... | collective-permute-start | bytes 2312 | tf_op jit(solution)/shard_map/ppermute | solution.py:23
  354.7 15.0 %collective-permute-start.32 = (f32[3,64]{1,0:T(4,128)S(1)}, f32[3,64]{1,0:T(4,128)S(1)}, u32[]{:S(2)}, u32[]{:S(2)}) collective-permute-start(f32[3,64]{1,0:T(4,128)S(1)} %get-tuple-element.93), channel_id=1, source_target_pairs={{0,1},{1,2},{2,3},{3,4},{4,5},{5,6},{6,7},{7,8},{8,9},{9,10},{10,1... | collective-permute-start | bytes 2312 | tf_op jit(solution)/shard_map/ppermute | solution.py:22
  356.6 13.1 %collective-permute-start.33 = (f32[3,64]{1,0:T(4,128)S(1)}, f32[3,64]{1,0:T(4,128)S(1)}, u32[]{:S(2)}, u32[]{:S(2)}) collective-permute-start(f32[3,64]{1,0:T(4,128)S(1)} %get-tuple-element.92), channel_id=1, source_target_pairs={{1,0},{2,1},{3,2},{4,3},{5,4},{6,5},{7,6},{8,7},{9,8},{10,9},{11,1... | collective-permute-start | bytes 2312 | tf_op jit(solution)/shard_map/ppermute | solution.py:23
  366.1 13.3 %all-to-all-start.5 = ((f32[128,1,384]{2,1,0:T(1,128)}), f32[128,1,384]{2,1,0:T(1,128)S(1)}, u32[]{:S(2)}, u32[]{:S(2)}) async-start(f32[128,1,384]{2,1,0:T(1,128)} %reshape.477), calls=%async_computation.5 | async-start | bytes 393216 | tf_op jit(solution)/shard_map/all_to_all | solution.py:184
  387.1 10.4 %collective-permute-start.28 = (f32[3,1,16]{1,2,0:T(8,128)S(1)}, f32[3,1,16]{1,2,0:T(8,128)S(1)}, u32[]{:S(2)}, u32[]{:S(2)}) collective-permute-start(f32[3,1,16]{1,2,0:T(8,128)S(1)} %get-tuple-element.66), channel_id=1, source_target_pairs={{32,0},{64,32},{96,64},{33,1},{65,33},{97,65},{34,2},{66,34},{98,6... | collective-permute-start | bytes 584 | tf_op jit(solution)/shard_map/ppermute | solution.py:60
  390.2 7.3 %collective-permute-start.29 = (f32[3,1,16]{1,2,0:T(8,128)S(1)}, f32[3,1,16]{1,2,0:T(8,128)S(1)}, u32[]{:S(2)}, u32[]{:S(2)}) collective-permute-start(f32[3,1,16]{1,2,0:T(8,128)S(1)} %get-tuple-element.67), channel_id=1, source_target_pairs={{0,32},{32,64},{64,96},{1,33},{33,65},{65,97},{2,34},{34,66},{66,9... | collective-permute-start | bytes 584 | tf_op jit(solution)/shard_map/ppermute | solution.py:59
  393.0 4.9 %collective-permute-start.30 = (f32[3,32,1]{1,2,0:T(1,128)S(1)}, f32[3,32,1]{1,2,0:T(1,128)S(1)}, u32[]{:S(2)}, u32[]{:S(2)}) collective-permute-start(f32[3,32,1]{1,2,0:T(1,128)S(1)} %get-tuple-element.70), channel_id=1, source_target_pairs={{1,0},{2,1},{3,2},{4,3},{5,4},{6,5},{7,6},{8,7},{9,8},{10,9},{11,1... | collective-permute-start | bytes 1160 | tf_op jit(solution)/shard_map/ppermute | solution.py:60
  394.3 3.8 collective-permute-start.31
  404.8 18.7 %all-to-all-start.6 = ((f32[128,1,384]{2,1,0:T(1,128)}), f32[128,1,384]{2,1,0:T(1,128)S(1)}, u32[]{:S(2)}, u32[]{:S(2)}) async-start(f32[128,1,384]{2,1,0:T(1,128)} %reshape.479), calls=%async_computation.6 | async-start | bytes 393216 | tf_op jit(solution)/shard_map/all_to_all | solution.py:119
  425.4 9.8 %collective-permute-start.34 = (f32[3,64]{1,0:T(4,128)S(1)}, f32[3,64]{1,0:T(4,128)S(1)}, u32[]{:S(2)}, u32[]{:S(2)}) collective-permute-start(f32[3,64]{1,0:T(4,128)S(1)} %get-tuple-element.91), channel_id=1, source_target_pairs={{0,1},{1,2},{2,3},{3,4},{4,5},{5,6},{6,7},{7,8},{8,9},{9,10},{10,1... | collective-permute-start | bytes 2312 | tf_op jit(solution)/shard_map/ppermute | solution.py:22
  427.3 9.2 %collective-permute-start.35 = (f32[3,64]{1,0:T(4,128)S(1)}, f32[3,64]{1,0:T(4,128)S(1)}, u32[]{:S(2)}, u32[]{:S(2)}) collective-permute-start(f32[3,64]{1,0:T(4,128)S(1)} %get-tuple-element.90), channel_id=1, source_target_pairs={{1,0},{2,1},{3,2},{4,3},{5,4},{6,5},{7,6},{8,7},{9,8},{10,9},{11,1... | collective-permute-start | bytes 2312 | tf_op jit(solution)/shard_map/ppermute | solution.py:23
  442.2 31.3 %collective-permute-start.36 = (f32[3,64]{1,0:T(4,128)S(1)}, f32[3,64]{1,0:T(4,128)S(1)}, u32[]{:S(2)}, u32[]{:S(2)}) collective-permute-start(f32[3,64]{1,0:T(4,128)S(1)} %get-tuple-element.89), channel_id=1, source_target_pairs={{0,1},{1,2},{2,3},{3,4},{4,5},{5,6},{6,7},{7,8},{8,9},{9,10},{10,1... | collective-permute-start | bytes 2312 | tf_op jit(solution)/shard_map/ppermute | solution.py:22
  444.2 29.4 %collective-permute-start.37 = (f32[3,64]{1,0:T(4,128)S(1)}, f32[3,64]{1,0:T(4,128)S(1)}, u32[]{:S(2)}, u32[]{:S(2)}) collective-permute-start(f32[3,64]{1,0:T(4,128)S(1)} %get-tuple-element.88), channel_id=1, source_target_pairs={{1,0},{2,1},{3,2},{4,3},{5,4},{6,5},{7,6},{8,7},{9,8},{10,9},{11,1... | collective-permute-start | bytes 2312 | tf_op jit(solution)/shard_map/ppermute | solution.py:23
  (25 other events, 353.9 us)

commit v2 on v1

--- a/solution.py
+++ b/solution.py
@@ -37,13 +37,27 @@
     laplace = (
         east_side + west_side + north_side + south_side + upper_side + lower_side - 6.0 * centre
     )
-    first_flux = jnp.einsum(
-        "cd,dxyz->cxyz", first_jacobian, 0.5 * (east_side - west_side), precision=HIGHEST
-    )
-    second_flux = jnp.einsum(
-        "cd,dxyz->cxyz", second_jacobian, 0.5 * (north_side - south_side), precision=HIGHEST
-    )
-    return diffusivity[None] * laplace - first_flux - second_flux
+    first_step = 0.5 * (east_side - west_side)
+    second_step = 0.5 * (north_side - south_side)
+    return (
+        diffusivity[None] * laplace
+        - blended(first_jacobian, first_step)
+        - blended(second_jacobian, second_step)
+    )
+
+
+def blended(jacobian, values):
+    total = jacobian[:, 0, None, None, None] * values[0][None]
+    for d in range(1, values.shape[0]):
+        total = total + jacobian[:, d, None, None, None] * values[d][None]
+    return total
+
+
+def mixed(jacobian, row, values):
+    total = jacobian[row, 0] * values[0]
+    for d in range(1, values.shape[0]):
+        total = total + jacobian[row, d] * values[d]
+    return total
 
 
 def face_rim(field):
@@ -163,18 +177,18 @@
         + TIME_STEP
         * homogeneous(face_rim(first_section), diffusivity, first_jacobian, second_jacobian)
     )
+    settled = lax.optimization_barrier(settled)
     settled_wall = settled[4, :, :, 0]
     half_square = 0.5 * TIME_STEP * TIME_STEP
+    edge_rows = jnp.array([1.0, 0.0, 0.0, 0.0, 1.0], jnp.float32)
 
     def wall_state(motion_plane):
         source = motion_plane * wall_bottom[None]
         (east_side, west_side), (north_side, south_side) = plane_sides(source)
-        first_flux = jnp.einsum(
-            "cd,dxy->cxy", first_jacobian[:, 1:4], 0.5 * (east_side - west_side), precision=HIGHEST
-        )
-        second_flux = jnp.einsum(
-            "cd,dxy->cxy", second_jacobian[:, 1:4], 0.5 * (north_side - south_side), precision=HIGHEST
-        )
+        first_step = 0.5 * (east_side - west_side)
+        second_step = 0.5 * (north_side - south_side)
+        first_flux = jnp.stack([mixed(first_jacobian[:, 1:4], c, first_step) for c in range(5)])
+        second_flux = jnp.stack([mixed(second_jacobian[:, 1:4], c, second_step) for c in range(5)])
         return source, east_side + west_side + north_side + south_side, first_flux, second_flux
 
     current = displacement
@@ -205,12 +219,11 @@
     above = half_square * wall_above[None] * source
     zero_plane = jnp.zeros_like(source[:1])
     bottom = jnp.concatenate([zero_plane, bottom, zero_plane], axis=0)
-    bottom = bottom.at[0].add(-half_square * (first_flux[0] + second_flux[0]))
-    bottom = bottom.at[4].add(-half_square * (first_flux[4] + second_flux[4]))
+    bottom = bottom - half_square * (first_flux + second_flux) * edge_rows[:, None, None]
     above = jnp.concatenate([zero_plane, above, zero_plane], axis=0)
-    edge = jnp.stack([bottom, above], axis=3)
-    fluid_field = lax.dynamic_update_slice(
-        settled, settled[:, :, :, 0:2] + edge, (0, 0, 0, 0)
+    depth = lax.broadcasted_iota(jnp.int32, settled.shape, 3)
+    fluid_field = settled + jnp.where(
+        depth == 0, bottom[..., None], jnp.where(depth == 1, above[..., None], 0.0)
     )
     return (fluid_field, current)
 

time: 490 us -> 749 us (1.53)
  other arithmetic: 11.6 us -> 247 us
  local copies, waits for them, and re-layouts: 77.9 us -> 179 us
  matrix products: 150 us -> 83.3 us
  waiting for transfers between devices: 36.9 us -> 27.9 us
    mul x6 -> x10, other arithmetic: 0.31 us -> 141 us  [the longest x2 67 us: homogeneous(): first_step = 0.5 * (east_side - west_side)]
    dot_general x10 -> x0, matrix products: 66.1 us -> none  [the longest x2 51.7 us: homogeneous(): jnp.einsum('cd,dxyz->cxyz', second_jacobian, 0.5 * (north_side - south_si...]
    add x1 -> x2, other arithmetic: 0.02 us -> 47.8 us  [the longest x1 36.9 us: local(): fluid_state + TIME_STEP * homogeneous(face_rim(fluid_state), diffusivity,...]
    mul x0 -> x4, local copies, waits for them, and re-layouts: none -> 25.8 us  [blended(): total = jacobian[:, 0, None, None, None] * values[0][None]]
    unnamed x74 -> x79, local copies, waits for them, and re-layouts: 25 us -> 49 us
    slice x3 -> x5, local copies, waits for them, and re-layouts: 2.66 us -> 24.5 us  [with_halo(): last = lax.slice_in_dim(array, length - width, length, axis=dim)]
    unnamed x0 -> x8, other arithmetic: none -> 19.8 us
    ppermute x0 -> x6, local copies, waits for them, and re-layouts: none -> 17.4 us  [the longest x3 9.93 us: with_halo(): before = lax.ppermute(last, axis, up)]
  transfers between devices with their start and end apart: 45 -> 45, of which waited for: 12 -> 11; matrix products, arithmetic and copies ran while one was open for 21% -> 36% of each run, Pallas kernels for 0% -> 0%
where the time goes in v2:
time: 749 us; the launch traced here: 740 us
  other arithmetic  247 us (33%)
  starting transfers between devices  200 us (27%)
  local copies, waits for them, and re-layouts  179 us (24%)
  matrix products  83.3 us (11%)
  waiting for transfers between devices  27.9 us (4%)
    ppermute x13, starting transfers between devices, with_halo(): after = lax.ppermute(first, axis, down)  78.6 us
    mul x2, other arithmetic, homogeneous(): first_step = 0.5 * (east_side - west_side)  67 us
    mul x1, other arithmetic, local(): 0.5 * (fluid_state + first_section + TIME_STEP * homogeneous(face_rim(fir...  60.7 us
    unnamed x79, local copies, waits for them, and re-layouts  49 us
    dot_general x9, matrix products, off_diagonal(): jnp.einsum('ibmn,ibcn->cim', stiff_tiles, chosen, precision=HIGHEST)  46.7 us
    add x1, other arithmetic, local(): fluid_state + TIME_STEP * homogeneous(face_rim(fluid_state), diffusivity,...  36.9 us
    all_to_all x3, starting transfers between devices, send_forth(): lax.all_to_all(buffer, ('sec', 'blk'), split_axis=0, concat_axis=0, tiled...  34.5 us
    ppermute x13, starting transfers between devices, with_halo(): before = lax.ppermute(last, axis, up)  32 us
  transfers between devices with their start and end apart: 45, of which 11 were waited for; matrix products, arithmetic and copies ran while one was open for 36% of the time, Pallas kernels for 0%

profile of v2, /device:TPU:32, one launch (start us, length us, event | category | flops | bytes accessed | tf_op | source)
XLA Modules:
  0.0 739.6 jit_solution(11265696819832273680)
XLA Ops:
  10.1 10.2 %all-to-all-start = ((s32[128,1,2]{2,1,0:T(1,128)}), s32[128,1,2]{2,1,0:T(1,128)S(1)}, u32[]{:S(2)}, u32[]{:S(2)}) async-start(s32[128,1,2]{2,1,0:T(1,128)} %bitcast.23), calls=%async_computation | async-start | bytes 131072 | tf_op jit(solution)/shard_map/all_to_all | solution.py:117
  23.1 7.7 %collective-permute-start.13 = (f32[3,64]{1,0:T(4,128)S(1)}, f32[3,64]{1,0:T(4,128)S(1)}, u32[]{:S(2)}, u32[]{:S(2)}) collective-permute-start(f32[3,64]{1,0:T(4,128)S(1)} %get-tuple-element.119), channel_id=1, source_target_pairs={{1,0},{2,1},{3,2},{4,3},{5,4},{6,5},{7,6},{8,7},{9,8},{10,9},{11,1... | collective-permute-start | bytes 2312 | tf_op jit(solution)/shard_map/ppermute | solution.py:23
  30.9 8.9 %copy.266 = f32[5,32,16,256]{1,2,3,0:T(8,128)} copy(f32[5,32,16,256]{3,2,1,0:T(8,128)} %param.14) | data formatting | bytes 5242880 | tf_op args[0]
  42.7 15.6 %fusion.122 = (f32[5,32,16,255]{1,2,3,0:T(8,128)}, f32[5,32,16,255]{1,2,3,0:T(8,128)}) fusion(f32[5,32,16,256]{1,2,3,0:T(8,128)} %copy.266), kind=kLoop, calls=%fused_computation.262 | loop fusion | bytes 10444800 | tf_op jit(solution)/shard_map/slice | solution.py:35
  64.7 5.5 all-to-all-start.1
  70.3 6.8 constant_dynamic-update-slice_fusion.1
  78.8 9.0 %copy.258 = f32[5,34,16,256]{1,2,3,0:T(8,128)} copy(f32[5,34,16,256]{3,2,1,0:T(8,128)} %copy-done.1) | data formatting | bytes 5570560 | tf_op jit(solution)/shard_map/concatenate | solution.py:24
  93.0 8.9 %copy.371 = f32[5,32,16,256]{1,2,3,0:T(8,128)} copy(f32[5,32,16,256]{3,2,1,0:T(8,128)} %get-tuple-element.72) | data formatting | bytes 5242880
  101.9 8.8 %copy.372 = f32[5,32,16,256]{1,2,3,0:T(8,128)} copy(f32[5,32,16,256]{3,2,1,0:T(8,128)} %get-tuple-element.73) | data formatting | bytes 5242880
  110.7 12.7 %subtract_multiply_fusion.3 = f32[5,32,16,256]{1,2,3,0:T(8,128)} fusion(f32[5,32,16,256]{1,2,3,0:T(8,128)} %copy.371, f32[5,32,16,256]{1,2,3,0:T(8,128)} %copy.372), kind=kLoop, calls=%fused_computation.16 | loop fusion | flops 1310720 | bytes 7864320 | tf_op jit(solution)/shard_map/mul | solution.py:40
  123.4 8.2 %slice_bitcast_fusion.19 = (f32[32,16,256]{0,1,2:T(8,128)}, f32[32,16,256]{0,1,2:T(8,128)}, f32[32,16,256]{0,1,2:T(8,128)}, f32[32,16,256]{0,1,2:T(8,128)}, f32[32,16,256]{0,1,2:T(8,128)}) fusion(f32[5,32,16,256]{1,2,3,0:T(8,128)} %subtract_multiply_fusion.3), kind=kLoop, calls=%fused_computation.38 | loop fusion | bytes 5242880 | tf_op jit(solution)/shard_map/mul | solution.py:50
  133.9 5.6 fusion.5
  154.9 12.4 %subtract_multiply_fusion.2 = f32[5,32,16,256]{1,2,3,0:T(8,128)S(1)} fusion(f32[5,34,1,256]{1,2,3,0:T(1,128)S(1)} %copy.259, f32[5,34,16,256]{1,2,3,0:T(8,128)} %copy.258, f32[5,34,1,256]{1,2,3,0:T(1,128)S(1)} %copy.260), kind=kLoop, calls=%fused_computation.15 | loop fusion | flops 2621440 | bytes 5754880 | tf_op jit(solution)/shard_map/mul | solution.py:41
  171.5 36.9 %multiply_add_fusion = f32[5,32,16,256]{1,2,3,0:T(8,128)} fusion(f32[5,32,16,256]{1,2,3,0:T(8,128)} %copy.266, f32[5,32,16,255]{1,2,3,0:T(8,128)} %get-tuple-element.68, f32[5,32,16,255]{1,2,3,0:T(8,128)} %get-tuple-element.67, f32[5,32,16,256]{1,2,3,0:T(8,128)} %copy.371, f32[5,32,16,256]{1,2,3,0:T(8,128)} %copy.372, f32[5,34,1,256]{1,2,3,0:T(1,128)S(1)} %copy.259, ...), kind=kLoop, calls=%fused_computation.14 | loop fusion | flops 20971520 | bytes 24608968 | tf_op jit(solution)/shard_map/add | solution.py:171
  208.3 16.2 %fusion.120 = (f32[5,1,16,256]{1,2,3,0:T(8,128)}, f32[5,1,16,256]{1,2,3,0:T(8,128)}) fusion(f32[5,32,16,256]{1,2,3,0:T(8,128)} %multiply_add_fusion), kind=kLoop, calls=%fused_computation.260 | loop fusion | bytes 327680 | tf_op jit(solution)/shard_map/slice | solution.py:20
  224.5 6.1 copy.267
  233.4 6.1 copy.269
  243.3 5.5 copy.268
  248.8 5.6 copy.270
  254.3 13.0 %pad_maximum_fusion.12 = (f32[5,34,1,256]{1,2,3,0:T(1,128)S(1)}, f32[5,34,1,256]{1,2,3,0:T(1,128)S(1)}) fusion(f32[5,1,16,256]{1,2,3,0:T(8,128)} %copy.268, f32[5,32,16,256]{1,2,3,0:T(8,128)} %multiply_add_fusion, f32[5,1,16,256]{1,2,3,0:T(8,128)} %copy.270), kind=kLoop, calls=%fused_computation.63 | loop fusion | flops 174080 | bytes 3133440 | tf_op jit(solution)/shard_map/concatenate | solution.py:24
  275.1 15.5 %fusion.121 = (f32[5,32,16,255]{1,2,3,0:T(8,128)}, f32[5,32,16,255]{1,2,3,0:T(8,128)}) fusion(f32[5,32,16,256]{1,2,3,0:T(8,128)} %multiply_add_fusion), kind=kLoop, calls=%fused_computation.261 | loop fusion | bytes 10444800 | tf_op jit(solution)/shard_map/slice | solution.py:35
  293.9 54.3 %subtract_multiply_fusion.1 = (f32[5,32,16,256]{1,2,3,0:T(8,128)}, f32[5,32,16,256]{1,2,3,0:T(8,128)}) fusion(f32[5,1,16,256]{1,2,3,0:T(8,128)} %copy.268, f32[5,32,16,256]{1,2,3,0:T(8,128)} %multiply_add_fusion, f32[5,1,16,256]{1,2,3,0:T(8,128)} %copy.270, f32[5,34,1,256]{1,2,3,0:T(1,128)S(1)} %copy.276, f32[5,34,1,256]{1,2,3,0:T(1,128)S(1)} %copy.274), kind=kLoop, calls=%fused_computation.13 | loop fusion | flops 7864320 | bytes 8376320 | tf_op jit(solution)/shard_map/mul | solution.py:40
  348.2 9.5 %slice_bitcast_fusion.9 = (f32[32,16,256]{0,1,2:T(8,128)}, f32[32,16,256]{0,1,2:T(8,128)}, f32[32,16,256]{0,1,2:T(8,128)}, f32[32,16,256]{0,1,2:T(8,128)}, f32[32,16,256]{0,1,2:T(8,128)}) fusion(f32[5,32,16,256]{1,2,3,0:T(8,128)} %get-tuple-element.39), kind=kLoop, calls=%fused_computation.28 | loop fusion | bytes 5242880 | tf_op jit(solution)/shard_map/mul | solution.py:50
  363.0 60.7 %add_multiply_fusion = f32[5,32,16,256]{1,2,3,0:T(8,128)} fusion(f32[5,32,16,256]{1,2,3,0:T(8,128)} %multiply_add_fusion, f32[5,32,16,255]{1,2,3,0:T(8,128)} %get-tuple-element.56, f32[5,32,16,255]{1,2,3,0:T(8,128)} %get-tuple-element.55, f32[5,32,16,256]{1,2,3,0:T(8,128)} %copy.266, f32[32,16,256]{0,1,2:T(8,128)} %get-tuple-element.49, ...), kind=kLoop, calls=%fused_computation.11 | loop fusion | flops 26214400 | bytes 19366088 | tf_op jit(solution)/shard_map/mul | solution.py:174
  434.5 16.3 %all-to-all-start.2 = ((f32[128,1,384]{2,1,0:T(1,128)}), f32[128,1,384]{2,1,0:T(1,128)S(1)}, u32[]{:S(2)}, u32[]{:S(2)}) async-start(f32[128,1,384]{2,1,0:T(1,128)} %reshape.559), calls=%async_computation.2 | async-start | bytes 393216 | tf_op jit(solution)/shard_map/all_to_all | solution.py:133
  450.8 5.7 convolution_bitcast_fusion.8
  464.4 7.9 %collective-permute-start.15 = (f32[3,64]{1,0:T(4,128)S(1)}, f32[3,64]{1,0:T(4,128)S(1)}, u32[]{:S(2)}, u32[]{:S(2)}) collective-permute-start(f32[3,64]{1,0:T(4,128)S(1)} %get-tuple-element.117), channel_id=1, source_target_pairs={{1,0},{2,1},{3,2},{4,3},{5,4},{6,5},{7,6},{8,7},{9,8},{10,9},{11,1... | collective-permute-start | bytes 2312 | tf_op jit(solution)/shard_map/ppermute | solution.py:23
  474.0 5.1 convolution_bitcast_fusion.7
  481.3 7.9 %collective-permute-start.17 = (f32[3,64]{1,0:T(4,128)S(1)}, f32[3,64]{1,0:T(4,128)S(1)}, u32[]{:S(2)}, u32[]{:S(2)}) collective-permute-start(f32[3,64]{1,0:T(4,128)S(1)} %get-tuple-element.115), channel_id=1, source_target_pairs={{1,0},{2,1},{3,2},{4,3},{5,4},{6,5},{7,6},{8,7},{9,8},{10,9},{11,1... | collective-permute-start | bytes 2312 | tf_op jit(solution)/shard_map/ppermute | solution.py:23
  490.9 5.1 convolution_bitcast_fusion.6
  498.2 8.3 %collective-permute-start.23 = (f32[3,64]{1,0:T(4,128)S(1)}, f32[3,64]{1,0:T(4,128)S(1)}, u32[]{:S(2)}, u32[]{:S(2)}) collective-permute-start(f32[3,64]{1,0:T(4,128)S(1)} %get-tuple-element.113), channel_id=1, source_target_pairs={{1,0},{2,1},{3,2},{4,3},{5,4},{6,5},{7,6},{8,7},{9,8},{10,9},{11,1... | collective-permute-start | bytes 2312 | tf_op jit(solution)/shard_map/ppermute | solution.py:23
  512.3 9.2 %all-to-all-done.3 = f32[128,1,384]{2,1,0:T(1,128)S(1)} async-done(((f32[128,1,384]{2,1,0:T(1,128)}), f32[128,1,384]{2,1,0:T(1,128)S(1)}, u32[]{:S(2)}, u32[]{:S(2)}) %all-to-all-start.3) | async-done | bytes 196640 | tf_op jit(solution)/shard_map/all_to_all | solution.py:198
  523.3 5.6 fusion.3
  551.0 9.2 %all-to-all-start.4 = ((f32[128,1,384]{2,1,0:T(1,128)}), f32[128,1,384]{2,1,0:T(1,128)S(1)}, u32[]{:S(2)}, u32[]{:S(2)}) async-start(f32[128,1,384]{2,1,0:T(1,128)} %reshape.563), calls=%async_computation.4 | async-start | bytes 393216 | tf_op jit(solution)/shard_map/all_to_all | solution.py:133
  560.2 5.1 convolution_bitcast_fusion.5
  573.7 7.9 %collective-permute-start.25 = (f32[3,64]{1,0:T(4,128)S(1)}, f32[3,64]{1,0:T(4,128)S(1)}, u32[]{:S(2)}, u32[]{:S(2)}) collective-permute-start(f32[3,64]{1,0:T(4,128)S(1)} %get-tuple-element.111), channel_id=1, source_target_pairs={{1,0},{2,1},{3,2},{4,3},{5,4},{6,5},{7,6},{8,7},{9,8},{10,9},{11,1... | collective-permute-start | bytes 2312 | tf_op jit(solution)/shard_map/ppermute | solution.py:23
  583.3 5.1 convolution_bitcast_fusion.4
  590.6 7.9 %collective-permute-start.27 = (f32[3,64]{1,0:T(4,128)S(1)}, f32[3,64]{1,0:T(4,128)S(1)}, u32[]{:S(2)}, u32[]{:S(2)}) collective-permute-start(f32[3,64]{1,0:T(4,128)S(1)} %get-tuple-element.109), channel_id=1, source_target_pairs={{1,0},{2,1},{3,2},{4,3},{5,4},{6,5},{7,6},{8,7},{9,8},{10,9},{11,1... | collective-permute-start | bytes 2312 | tf_op jit(solution)/shard_map/ppermute | solution.py:23
  600.2 5.1 convolution_bitcast_fusion.3
  607.5 7.9 %collective-permute-start.33 = (f32[3,64]{1,0:T(4,128)S(1)}, f32[3,64]{1,0:T(4,128)S(1)}, u32[]{:S(2)}, u32[]{:S(2)}) collective-permute-start(f32[3,64]{1,0:T(4,128)S(1)} %get-tuple-element.107), channel_id=1, source_target_pairs={{1,0},{2,1},{3,2},{4,3},{5,4},{6,5},{7,6},{8,7},{9,8},{10,9},{11,1... | collective-permute-start | bytes 2312 | tf_op jit(solution)/shard_map/ppermute | solution.py:23
  621.4 5.1 convolution_bitcast_fusion.2
  632.4 5.6 fusion.1
  649.4 6.2 subtract_bitcast_fusion
  661.9 9.0 %all-to-all-start.6 = ((f32[128,1,384]{2,1,0:T(1,128)}), f32[128,1,384]{2,1,0:T(1,128)S(1)}, u32[]{:S(2)}, u32[]{:S(2)}) async-start(f32[128,1,384]{2,1,0:T(1,128)} %reshape.567), calls=%async_computation.6 | async-start | bytes 393216 | tf_op jit(solution)/shard_map/all_to_all | solution.py:133
  688.0 8.0 %collective-permute-start.35 = (f32[3,64]{1,0:T(4,128)S(1)}, f32[3,64]{1,0:T(4,128)S(1)}, u32[]{:S(2)}, u32[]{:S(2)}) collective-permute-start(f32[3,64]{1,0:T(4,128)S(1)} %get-tuple-element.105), channel_id=1, source_target_pairs={{1,0},{2,1},{3,2},{4,3},{5,4},{6,5},{7,6},{8,7},{9,8},{10,9},{11,1... | collective-permute-start | bytes 2312 | tf_op jit(solution)/shard_map/ppermute | solution.py:23
  704.8 7.9 %collective-permute-start.37 = (f32[3,64]{1,0:T(4,128)S(1)}, f32[3,64]{1,0:T(4,128)S(1)}, u32[]{:S(2)}, u32[]{:S(2)}) collective-permute-start(f32[3,64]{1,0:T(4,128)S(1)} %get-tuple-element.103), channel_id=1, source_target_pairs={{1,0},{2,1},{3,2},{4,3},{5,4},{6,5},{7,6},{8,7},{9,8},{10,9},{11,1... | collective-permute-start | bytes 2312 | tf_op jit(solution)/shard_map/ppermute | solution.py:23
  712.7 11.0 %select_add_fusion = f32[5,32,16,256]{1,2,3,0:T(8,128)} fusion(f32[5,32,16,256]{1,2,3,0:T(8,128)} %add_multiply_fusion, f32[5,32,16]{1,2,0:T(8,128)S(1)} %get-tuple-element.122, f32[5,32,16]{1,2,0:T(8,128)S(1)} %get-tuple-element.121, pred[256]{0:T(512)(128)(4,1)S(1)} %get-tuple-element.164, pred[256]{0:T(512)(128)(4,1)S(1)} %get-tuple-element.165), kind=kLoop, calls=%fused_computation.10 | loop fusion | flops 1966080 | bytes 5263872 | tf_op jit(solution)/shard_map/add | solution.py:225
  723.6 9.4 %copy.336 = f32[5,32,16,256]{3,2,1,0:T(8,128)} copy(f32[5,32,16,256]{1,2,3,0:T(8,128)} %select_add_fusion) | data formatting | bytes 5242880
  (337 shorter events, 205.3 us)
Async XLA Ops:
  1.6 68.6 %collective-permute-start.1 = (f32[5,1,16,256]{3,2,1,0:T(8,128)S(1)}, f32[5,1,16,256]{3,2,1,0:T(8,128)S(1)}, u32[]{:S(2)}, u32[]{:S(2)}) collective-permute-start(f32[5,1,16,256]{3,2,1,0:T(8,128)S(1)} %get-tuple-element.74), channel_id=1, source_target_pairs={{0,32},{32,64},{64,96},{1,33},{33,65},{65,97},{2,34},{34,66},{66,9... | collective-permute-start | bytes 245768 | tf_op jit(solution)/shard_map/ppermute | solution.py:22
  5.4 64.8 %collective-permute-start = (f32[5,1,16,256]{3,2,1,0:T(8,128)S(1)}, f32[5,1,16,256]{3,2,1,0:T(8,128)S(1)}, u32[]{:S(2)}, u32[]{:S(2)}) collective-permute-start(f32[5,1,16,256]{3,2,1,0:T(8,128)S(1)} %get-tuple-element.75), channel_id=1, source_target_pairs={{32,0},{64,32},{96,64},{33,1},{65,33},{97,65},{34,2},{66,34},{98,6... | collective-permute-start | bytes 245768 | tf_op jit(solution)/shard_map/ppermute | solution.py:23
  10.1 52.3 %all-to-all-start = ((s32[128,1,2]{2,1,0:T(1,128)}), s32[128,1,2]{2,1,0:T(1,128)S(1)}, u32[]{:S(2)}, u32[]{:S(2)}) async-start(s32[128,1,2]{2,1,0:T(1,128)} %bitcast.23), calls=%async_computation | async-start | bytes 131072 | tf_op jit(solution)/shard_map/all_to_all | solution.py:117
  21.1 40.1 %collective-permute-start.12 = (f32[3,64]{1,0:T(4,128)S(1)}, f32[3,64]{1,0:T(4,128)S(1)}, u32[]{:S(2)}, u32[]{:S(2)}) collective-permute-start(f32[3,64]{1,0:T(4,128)S(1)} %get-tuple-element.120), channel_id=1, source_target_pairs={{0,1},{1,2},{2,3},{3,4},{4,5},{5,6},{6,7},{7,8},{8,9},{9,10},{10,1... | collective-permute-start | bytes 2312 | tf_op jit(solution)/shard_map/ppermute | solution.py:22
  23.1 38.1 %collective-permute-start.13 = (f32[3,64]{1,0:T(4,128)S(1)}, f32[3,64]{1,0:T(4,128)S(1)}, u32[]{:S(2)}, u32[]{:S(2)}) collective-permute-start(f32[3,64]{1,0:T(4,128)S(1)} %get-tuple-element.119), channel_id=1, source_target_pairs={{1,0},{2,1},{3,2},{4,3},{5,4},{6,5},{7,6},{8,7},{9,8},{10,9},{11,1... | collective-permute-start | bytes 2312 | tf_op jit(solution)/shard_map/ppermute | solution.py:23
  41.4 130.0 %copy-start.20 = (f32[5]{0:T(128)}, f32[5]{0:T(128)S(1)}, u32[]{:S(2)}) copy-start(f32[5]{0:T(128)S(1)} %get-tuple-element.160) | copy-start | bytes 64
  41.4 130.0 %copy-start.22 = (f32[5]{0:T(128)}, f32[5]{0:T(128)S(1)}, u32[]{:S(2)}) copy-start(f32[5]{0:T(128)S(1)} %get-tuple-element.161) | copy-start | bytes 64
  64.7 66.9 %all-to-all-start.1 = ((f32[128,1,384]{2,1,0:T(1,128)}), f32[128,1,384]{2,1,0:T(1,128)S(1)}, u32[]{:S(2)}, u32[]{:S(2)}) async-start(f32[128,1,384]{2,1,0:T(1,128)} %reshape.557), calls=%async_computation.1 | async-start | bytes 393216 | tf_op jit(solution)/shard_map/all_to_all | solution.py:198
  87.8 63.9 %collective-permute-start.2 = (f32[5,34,1,256]{3,2,1,0:T(1,128)S(1)}, f32[5,34,1,256]{3,2,1,0:T(1,128)S(1)}, u32[]{:S(2)}, u32[]{:S(2)}) collective-permute-start(f32[5,34,1,256]{3,2,1,0:T(1,128)S(1)} %get-tuple-element.70), channel_id=1, source_target_pairs={{1,0},{2,1},{3,2},{4,3},{5,4},{6,5},{7,6},{8,7},{9,8},{10,9},{11,1... | collective-permute-start | bytes 522248 | tf_op jit(solution)/shard_map/ppermute | solution.py:23
  89.1 63.6 %collective-permute-start.3 = (f32[5,34,1,256]{3,2,1,0:T(1,128)S(1)}, f32[5,34,1,256]{3,2,1,0:T(1,128)}, u32[]{:S(2)}, u32[]{:S(2)}) collective-permute-start(f32[5,34,1,256]{3,2,1,0:T(1,128)S(1)} %get-tuple-element.69), channel_id=1, source_target_pairs={{0,1},{1,2},{2,3},{3,4},{4,5},{5,6},{6,7},{7,8},{8,9},{9,10},{10,1... | collective-permute-start | bytes 522248 | tf_op jit(solution)/shard_map/ppermute | solution.py:22
  140.4 7.1 collective-permute-start.8
  143.3 8.3 %collective-permute-start.9 = (f32[3,1,16]{1,2,0:T(8,128)S(1)}, f32[3,1,16]{1,2,0:T(8,128)S(1)}, u32[]{:S(2)}, u32[]{:S(2)}) collective-permute-start(f32[3,1,16]{1,2,0:T(8,128)S(1)} %get-tuple-element.95), channel_id=1, source_target_pairs={{0,32},{32,64},{64,96},{1,33},{33,65},{65,97},{2,34},{34,66},{66,9... | collective-permute-start | bytes 584 | tf_op jit(solution)/shard_map/ppermute | solution.py:73
  146.3 96.3 %collective-permute-start.10 = (f32[3,32,1]{1,2,0:T(1,128)}, f32[3,32,1]{1,2,0:T(1,128)}, u32[]{:S(2)}, u32[]{:S(2)}) collective-permute-start(f32[3,32,1]{1,2,0:T(1,128)} %get-tuple-element.100), channel_id=1, source_target_pairs={{1,0},{2,1},{3,2},{4,3},{5,4},{6,5},{7,6},{8,7},{9,8},{10,9},{11,1... | collective-permute-start | bytes 1160 | tf_op jit(solution)/shard_map/ppermute | solution.py:74
  147.6 95.0 %collective-permute-start.11 = (f32[3,32,1]{1,2,0:T(1,128)}, f32[3,32,1]{1,2,0:T(1,128)}, u32[]{:S(2)}, u32[]{:S(2)}) collective-permute-start(f32[3,32,1]{1,2,0:T(1,128)} %get-tuple-element.99), channel_id=1, source_target_pairs={{0,1},{1,2},{2,3},{3,4},{4,5},{5,6},{6,7},{7,8},{8,9},{9,10},{10,1... | collective-permute-start | bytes 1160 | tf_op jit(solution)/shard_map/ppermute | solution.py:73
  230.6 12.7 %collective-permute-start.4 = (f32[5,1,16,256]{3,2,1,0:T(8,128)S(1)}, f32[5,1,16,256]{3,2,1,0:T(8,128)S(1)}, u32[]{:S(2)}, u32[]{:S(2)}) collective-permute-start(f32[5,1,16,256]{3,2,1,0:T(8,128)S(1)} %copy.267), channel_id=1, source_target_pairs={{32,0},{64,32},{96,64},{33,1},{65,33},{97,65},{34,2},{66,34},{98,6... | collective-permute-start | bytes 245768 | tf_op jit(solution)/shard_map/ppermute | solution.py:23
  239.6 9.2 %collective-permute-start.5 = (f32[5,1,16,256]{3,2,1,0:T(8,128)S(1)}, f32[5,1,16,256]{3,2,1,0:T(8,128)S(1)}, u32[]{:S(2)}, u32[]{:S(2)}) collective-permute-start(f32[5,1,16,256]{3,2,1,0:T(8,128)S(1)} %copy.269), channel_id=1, source_target_pairs={{0,32},{32,64},{64,96},{1,33},{33,65},{65,97},{2,34},{34,66},{66,9... | collective-permute-start | bytes 245768 | tf_op jit(solution)/shard_map/ppermute | solution.py:22
  269.0 21.7 %collective-permute-start.6 = (f32[5,34,1,256]{3,2,1,0:T(1,128)}, f32[5,34,1,256]{3,2,1,0:T(1,128)S(1)}, u32[]{:S(2)}, u32[]{:S(2)}) collective-permute-start(f32[5,34,1,256]{3,2,1,0:T(1,128)} %copy.273), channel_id=1, source_target_pairs={{1,0},{2,1},{3,2},{4,3},{5,4},{6,5},{7,6},{8,7},{9,8},{10,9},{11,1... | collective-permute-start | bytes 522248 | tf_op jit(solution)/shard_map/ppermute | solution.py:23
  271.3 20.4 %collective-permute-start.7 = (f32[5,34,1,256]{3,2,1,0:T(1,128)S(1)}, f32[5,34,1,256]{3,2,1,0:T(1,128)}, u32[]{:S(2)}, u32[]{:S(2)}) collective-permute-start(f32[5,34,1,256]{3,2,1,0:T(1,128)S(1)} %copy.275), channel_id=1, source_target_pairs={{0,1},{1,2},{2,3},{3,4},{4,5},{5,6},{6,7},{7,8},{8,9},{9,10},{10,1... | collective-permute-start | bytes 522248 | tf_op jit(solution)/shard_map/ppermute | solution.py:22
  434.5 26.1 %all-to-all-start.2 = ((f32[128,1,384]{2,1,0:T(1,128)}), f32[128,1,384]{2,1,0:T(1,128)S(1)}, u32[]{:S(2)}, u32[]{:S(2)}) async-start(f32[128,1,384]{2,1,0:T(1,128)} %reshape.559), calls=%async_computation.2 | async-start | bytes 393216 | tf_op jit(solution)/shard_map/all_to_all | solution.py:133
  462.5 9.8 %collective-permute-start.14 = (f32[3,64]{1,0:T(4,128)S(1)}, f32[3,64]{1,0:T(4,128)S(1)}, u32[]{:S(2)}, u32[]{:S(2)}) collective-permute-start(f32[3,64]{1,0:T(4,128)S(1)} %get-tuple-element.118), channel_id=1, source_target_pairs={{0,1},{1,2},{2,3},{3,4},{4,5},{5,6},{6,7},{7,8},{8,9},{9,10},{10,1... | collective-permute-start | bytes 2312 | tf_op jit(solution)/shard_map/ppermute | solution.py:22
  464.4 9.2 %collective-permute-start.15 = (f32[3,64]{1,0:T(4,128)S(1)}, f32[3,64]{1,0:T(4,128)S(1)}, u32[]{:S(2)}, u32[]{:S(2)}) collective-permute-start(f32[3,64]{1,0:T(4,128)S(1)} %get-tuple-element.117), channel_id=1, source_target_pairs={{1,0},{2,1},{3,2},{4,3},{5,4},{6,5},{7,6},{8,7},{9,8},{10,9},{11,1... | collective-permute-start | bytes 2312 | tf_op jit(solution)/shard_map/ppermute | solution.py:23
  479.4 9.8 %collective-permute-start.16 = (f32[3,64]{1,0:T(4,128)S(1)}, f32[3,64]{1,0:T(4,128)S(1)}, u32[]{:S(2)}, u32[]{:S(2)}) collective-permute-start(f32[3,64]{1,0:T(4,128)S(1)} %get-tuple-element.116), channel_id=1, source_target_pairs={{0,1},{1,2},{2,3},{3,4},{4,5},{5,6},{6,7},{7,8},{8,9},{9,10},{10,1... | collective-permute-start | bytes 2312 | tf_op jit(solution)/shard_map/ppermute | solution.py:22
  481.3 9.2 %collective-permute-start.17 = (f32[3,64]{1,0:T(4,128)S(1)}, f32[3,64]{1,0:T(4,128)S(1)}, u32[]{:S(2)}, u32[]{:S(2)}) collective-permute-start(f32[3,64]{1,0:T(4,128)S(1)} %get-tuple-element.115), channel_id=1, source_target_pairs={{1,0},{2,1},{3,2},{4,3},{5,4},{6,5},{7,6},{8,7},{9,8},{10,9},{11,1... | collective-permute-start | bytes 2312 | tf_op jit(solution)/shard_map/ppermute | solution.py:23
  496.3 15.4 %collective-permute-start.22 = (f32[3,64]{1,0:T(4,128)S(1)}, f32[3,64]{1,0:T(4,128)S(1)}, u32[]{:S(2)}, u32[]{:S(2)}) collective-permute-start(f32[3,64]{1,0:T(4,128)S(1)} %get-tuple-element.114), channel_id=1, source_target_pairs={{0,1},{1,2},{2,3},{3,4},{4,5},{5,6},{6,7},{7,8},{8,9},{9,10},{10,1... | collective-permute-start | bytes 2312 | tf_op jit(solution)/shard_map/ppermute | solution.py:22
  498.2 13.5 %collective-permute-start.23 = (f32[3,64]{1,0:T(4,128)S(1)}, f32[3,64]{1,0:T(4,128)S(1)}, u32[]{:S(2)}, u32[]{:S(2)}) collective-permute-start(f32[3,64]{1,0:T(4,128)S(1)} %get-tuple-element.113), channel_id=1, source_target_pairs={{1,0},{2,1},{3,2},{4,3},{5,4},{6,5},{7,6},{8,7},{9,8},{10,9},{11,1... | collective-permute-start | bytes 2312 | tf_op jit(solution)/shard_map/ppermute | solution.py:23
  508.2 13.3 %all-to-all-start.3 = ((f32[128,1,384]{2,1,0:T(1,128)}), f32[128,1,384]{2,1,0:T(1,128)S(1)}, u32[]{:S(2)}, u32[]{:S(2)}) async-start(f32[128,1,384]{2,1,0:T(1,128)} %reshape.561), calls=%async_computation.3 | async-start | bytes 393216 | tf_op jit(solution)/shard_map/all_to_all | solution.py:198
  529.3 10.2 %collective-permute-start.18 = (f32[3,1,16]{1,2,0:T(8,128)S(1)}, f32[3,1,16]{1,2,0:T(8,128)S(1)}, u32[]{:S(2)}, u32[]{:S(2)}) collective-permute-start(f32[3,1,16]{1,2,0:T(8,128)S(1)} %get-tuple-element.88), channel_id=1, source_target_pairs={{32,0},{64,32},{96,64},{33,1},{65,33},{97,65},{34,2},{66,34},{98,6... | collective-permute-start | bytes 584 | tf_op jit(solution)/shard_map/ppermute | solution.py:74
  532.4 7.1 collective-permute-start.19
  535.1 4.5 collective-permute-start.20
  536.4 3.8 collective-permute-start.21
  551.0 18.9 %all-to-all-start.4 = ((f32[128,1,384]{2,1,0:T(1,128)}), f32[128,1,384]{2,1,0:T(1,128)S(1)}, u32[]{:S(2)}, u32[]{:S(2)}) async-start(f32[128,1,384]{2,1,0:T(1,128)} %reshape.563), calls=%async_computation.4 | async-start | bytes 393216 | tf_op jit(solution)/shard_map/all_to_all | solution.py:133
  571.8 9.8 %collective-permute-start.24 = (f32[3,64]{1,0:T(4,128)S(1)}, f32[3,64]{1,0:T(4,128)S(1)}, u32[]{:S(2)}, u32[]{:S(2)}) collective-permute-start(f32[3,64]{1,0:T(4,128)S(1)} %get-tuple-element.112), channel_id=1, source_target_pairs={{0,1},{1,2},{2,3},{3,4},{4,5},{5,6},{6,7},{7,8},{8,9},{9,10},{10,1... | collective-permute-start | bytes 2312 | tf_op jit(solution)/shard_map/ppermute | solution.py:22
  573.7 9.2 %collective-permute-start.25 = (f32[3,64]{1,0:T(4,128)S(1)}, f32[3,64]{1,0:T(4,128)S(1)}, u32[]{:S(2)}, u32[]{:S(2)}) collective-permute-start(f32[3,64]{1,0:T(4,128)S(1)} %get-tuple-element.111), channel_id=1, source_target_pairs={{1,0},{2,1},{3,2},{4,3},{5,4},{6,5},{7,6},{8,7},{9,8},{10,9},{11,1... | collective-permute-start | bytes 2312 | tf_op jit(solution)/shard_map/ppermute | solution.py:23
  588.7 9.8 %collective-permute-start.26 = (f32[3,64]{1,0:T(4,128)S(1)}, f32[3,64]{1,0:T(4,128)S(1)}, u32[]{:S(2)}, u32[]{:S(2)}) collective-permute-start(f32[3,64]{1,0:T(4,128)S(1)} %get-tuple-element.110), channel_id=1, source_target_pairs={{0,1},{1,2},{2,3},{3,4},{4,5},{5,6},{6,7},{7,8},{8,9},{9,10},{10,1... | collective-permute-start | bytes 2312 | tf_op jit(solution)/shard_map/ppermute | solution.py:22
  590.6 9.2 %collective-permute-start.27 = (f32[3,64]{1,0:T(4,128)S(1)}, f32[3,64]{1,0:T(4,128)S(1)}, u32[]{:S(2)}, u32[]{:S(2)}) collective-permute-start(f32[3,64]{1,0:T(4,128)S(1)} %get-tuple-element.109), channel_id=1, source_target_pairs={{1,0},{2,1},{3,2},{4,3},{5,4},{6,5},{7,6},{8,7},{9,8},{10,9},{11,1... | collective-permute-start | bytes 2312 | tf_op jit(solution)/shard_map/ppermute | solution.py:23
  605.6 15.3 %collective-permute-start.32 = (f32[3,64]{1,0:T(4,128)S(1)}, f32[3,64]{1,0:T(4,128)S(1)}, u32[]{:S(2)}, u32[]{:S(2)}) collective-permute-start(f32[3,64]{1,0:T(4,128)S(1)} %get-tuple-element.108), channel_id=1, source_target_pairs={{0,1},{1,2},{2,3},{3,4},{4,5},{5,6},{6,7},{7,8},{8,9},{9,10},{10,1... | collective-permute-start | bytes 2312 | tf_op jit(solution)/shard_map/ppermute | solution.py:22
  607.5 13.4 %collective-permute-start.33 = (f32[3,64]{1,0:T(4,128)S(1)}, f32[3,64]{1,0:T(4,128)S(1)}, u32[]{:S(2)}, u32[]{:S(2)}) collective-permute-start(f32[3,64]{1,0:T(4,128)S(1)} %get-tuple-element.107), channel_id=1, source_target_pairs={{1,0},{2,1},{3,2},{4,3},{5,4},{6,5},{7,6},{8,7},{9,8},{10,9},{11,1... | collective-permute-start | bytes 2312 | tf_op jit(solution)/shard_map/ppermute | solution.py:23
  617.1 13.5 %all-to-all-start.5 = ((f32[128,1,384]{2,1,0:T(1,128)}), f32[128,1,384]{2,1,0:T(1,128)S(1)}, u32[]{:S(2)}, u32[]{:S(2)}) async-start(f32[128,1,384]{2,1,0:T(1,128)} %reshape.565), calls=%async_computation.5 | async-start | bytes 393216 | tf_op jit(solution)/shard_map/all_to_all | solution.py:198
  621.4 74.7 %copy-start.29 = (f32[5]{0:T(128)S(1)}, f32[5]{0:T(128)}, u32[]{:S(2)}) copy-start(f32[5]{0:T(128)} %constant.53) | copy-start | bytes 64
  638.4 10.2 %collective-permute-start.28 = (f32[3,1,16]{1,2,0:T(8,128)S(1)}, f32[3,1,16]{1,2,0:T(8,128)S(1)}, u32[]{:S(2)}, u32[]{:S(2)}) collective-permute-start(f32[3,1,16]{1,2,0:T(8,128)S(1)} %get-tuple-element.85), channel_id=1, source_target_pairs={{32,0},{64,32},{96,64},{33,1},{65,33},{97,65},{34,2},{66,34},{98,6... | collective-permute-start | bytes 584 | tf_op jit(solution)/shard_map/ppermute | solution.py:74
  641.5 7.1 collective-permute-start.29
  644.2 4.5 collective-permute-start.30
  645.5 3.8 collective-permute-start.31
  661.9 22.2 %all-to-all-start.6 = ((f32[128,1,384]{2,1,0:T(1,128)}), f32[128,1,384]{2,1,0:T(1,128)S(1)}, u32[]{:S(2)}, u32[]{:S(2)}) async-start(f32[128,1,384]{2,1,0:T(1,128)} %reshape.567), calls=%async_computation.6 | async-start | bytes 393216 | tf_op jit(solution)/shard_map/all_to_all | solution.py:133
  686.0 10.1 %collective-permute-start.34 = (f32[3,64]{1,0:T(4,128)S(1)}, f32[3,64]{1,0:T(4,128)S(1)}, u32[]{:S(2)}, u32[]{:S(2)}) collective-permute-start(f32[3,64]{1,0:T(4,128)S(1)} %get-tuple-element.106), channel_id=1, source_target_pairs={{0,1},{1,2},{2,3},{3,4},{4,5},{5,6},{6,7},{7,8},{8,9},{9,10},{10,1... | collective-permute-start | bytes 2312 | tf_op jit(solution)/shard_map/ppermute | solution.py:22
  688.0 9.0 %collective-permute-start.35 = (f32[3,64]{1,0:T(4,128)S(1)}, f32[3,64]{1,0:T(4,128)S(1)}, u32[]{:S(2)}, u32[]{:S(2)}) collective-permute-start(f32[3,64]{1,0:T(4,128)S(1)} %get-tuple-element.105), channel_id=1, source_target_pairs={{1,0},{2,1},{3,2},{4,3},{5,4},{6,5},{7,6},{8,7},{9,8},{10,9},{11,1... | collective-permute-start | bytes 2312 | tf_op jit(solution)/shard_map/ppermute | solution.py:23
  702.9 30.1 %collective-permute-start.36 = (f32[3,64]{1,0:T(4,128)S(1)}, f32[3,64]{1,0:T(4,128)S(1)}, u32[]{:S(2)}, u32[]{:S(2)}) collective-permute-start(f32[3,64]{1,0:T(4,128)S(1)} %get-tuple-element.104), channel_id=1, source_target_pairs={{0,1},{1,2},{2,3},{3,4},{4,5},{5,6},{6,7},{7,8},{8,9},{9,10},{10,1... | collective-permute-start | bytes 2312 | tf_op jit(solution)/shard_map/ppermute | solution.py:22
  704.8 28.2 %collective-permute-start.37 = (f32[3,64]{1,0:T(4,128)S(1)}, f32[3,64]{1,0:T(4,128)S(1)}, u32[]{:S(2)}, u32[]{:S(2)}) collective-permute-start(f32[3,64]{1,0:T(4,128)S(1)} %get-tuple-element.103), channel_id=1, source_target_pairs={{1,0},{2,1},{3,2},{4,3},{5,4},{6,5},{7,6},{8,7},{9,8},{10,9},{11,1... | collective-permute-start | bytes 2312 | tf_op jit(solution)/shard_map/ppermute | solution.py:23
  (27 other events, 759.9 us)
